TPU v7x, 256 devices: a whole 4x4x8 slice. The times are simulated.
256 devices in a mesh: traj: 64 (over z, y, core), mstate: 4 (over x).
Axes of the slice: x: 4, y: 4, z: 8, core: 2. Of those that a mesh axis runs over, the one named last changes fastest.
Arguments:
- bias: float32 [32, 2097152], P(None, ('traj', 'mstate')), may hold values from -206 to 206
- labels: int32 [2097152], P(('traj', 'mstate')), may hold values from 0 to 4095, as said below
- therm_index: int32 [2097152], P(('traj', 'mstate')), may hold values from 0 to 31
- counts: int32 [32, 4096, 4096], P(None, 'traj', 'mstate'), may hold values from 0 to 4, as said below
- free_start: float32 [32, 4096], replicated, may hold values from -6 to 6
- mult_start: float32 [32, 4096], replicated, may hold values from -6 to 6
Outputs:
- free_energy: float32 [32, 4096], P(None, 'mstate')
- log_mult: float32 [32, 4096], P(None, 'mstate')
Inputs may be any that keep to these rules, and one draw needn't show every extreme that they name: `labels`: every Markov state is the label of at least one frame. `counts`: most entries are zero.
All inputs are finite; a program needn't handle non-finite values.
Results may differ from a plain program's by a relative error of at most 0.0001.
Values sent between devices are 32-bit elements; how exact they have to be, the bound alone decides.
No kernel may reach another device: no remote copies, remote signals or barrier semaphores. Data moves between devices by JAX's collectives and lax.ppermute only.
A program may use at most 64 MiB of HBM per device.

v0:
```python
import jax
import jax.numpy as jnp
from jax import lax
from jax.sharding import PartitionSpec as P

ITERS = 2


def per_device(bias, labels, therm_index, counts, free_start, mult_start):
    states_k = bias.shape[0]
    width = free_start.shape[1]
    col_count = counts.shape[1]
    row_count = counts.shape[2]
    col_start = lax.axis_index("traj") * col_count
    row_start = lax.axis_index("mstate") * row_count
    states = jax.nn.one_hot(therm_index, states_k, dtype=jnp.float32)
    local_visits = jax.ops.segment_sum(states, labels, num_segments=width).T
    visits = lax.psum(local_visits, ("traj", "mstate"))
    counts_real = counts.astype(jnp.float32)
    free, mult = (free_start, mult_start)
    for step in range(ITERS):
        free_cols = lax.dynamic_slice_in_dim(free, col_start, col_count, 1)
        mult_cols = lax.dynamic_slice_in_dim(mult, col_start, col_count, 1)
        free_rows = lax.dynamic_slice_in_dim(free, row_start, row_count, 1)
        mult_rows = lax.dynamic_slice_in_dim(mult, row_start, row_count, 1)
        weight = jax.nn.sigmoid(
            mult_rows[:, None, :]
            + free_cols[:, :, None]
            - mult_cols[:, :, None]
            - free_rows[:, None, :]
        )
        partial_rows = jnp.sum(counts_real * weight, axis=1)
        row_total = lax.psum(partial_rows, "traj")
        mult = lax.all_gather(jnp.log(0.5 + row_total), "mstate", axis=1, tiled=True)
        level = jnp.log(jnp.exp(mult) + visits) + free
        scores = jnp.take(level, labels, axis=1) - bias
        top = jnp.max(scores, axis=0)
        logl = top + jnp.log(jnp.sum(jnp.exp(scores - top[None, :]), axis=0))
        term = -bias - logl[None, :]
        shift = lax.pmax(jnp.max(term, axis=1), ("traj", "mstate"))
        weights = jnp.exp(term - shift[:, None])
        local_total = jax.ops.segment_sum(weights.T, labels, num_segments=width).T
        total = lax.psum(local_total, ("traj", "mstate"))
        free = -(shift[:, None] + jnp.log(total))
    free_out = lax.dynamic_slice_in_dim(free, row_start, row_count, 1)
    mult_out = lax.dynamic_slice_in_dim(mult, row_start, row_count, 1)
    return (free_out, mult_out)


def solution(mesh):
    placed = (
        P(None, ("traj", "mstate")),
        P(("traj", "mstate")),
        P(("traj", "mstate")),
        P(None, "traj", "mstate"),
        P(),
        P(),
    )
    return jax.shard_map(
        per_device,
        mesh=mesh,
        in_specs=placed,
        out_specs=(P(None, "mstate"), P(None, "mstate")),
        check_vma=False,
    )
```

profile of v0, /device:TPU:1, one launch (start us, length us, event | category | flops | bytes accessed | tf_op | source)
XLA Modules:
  0.0 1500.5 jit_solution(12562265268010864750)
XLA Ops:
  9.1 6.6 multiply_reduce_fusion.1
  15.8 48.6 %scatter_custom_fusion = f32[4096,32]{1,0:T(8,128)S(1)} fusion(s32[8192]{0:T(1024)S(1)} %copy-done.10, s32[8192]{0:T(1024)S(1)} %copy-done.11, f32[]{:T(128)} %constant.11.clone.1), kind=kCustom, calls=%fused_computation.11 | custom fusion | flops 786432 | bytes 557060 | tf_op jit(solution)/shard_map/scatter-add | solution.py:17
  65.9 2.6 copy.44
  68.5 127.5 %all-reduce.6.cloned.1.call-done = f32[32,1024]{1,0:T(8,128)} async-done(((f32[32,1024]{1,0:T(8,128)}), f32[32,1024]{1,0:T(8,128)}) %all-reduce.6.cloned.1.call-update) | async-done | bytes 131088 | tf_op jit(solution)/shard_map/psum | solution.py:33
  197.0 12.1 all_gather.6
  209.1 243.4 %all-reduce.8.cloned.1.call-done = f32[32,4096]{1,0:T(8,128)} async-done(((f32[32,4096]{1,0:T(8,128)}), f32[32,4096]{1,0:T(8,128)}) %all-reduce.8.cloned.1.call-update) | async-done | bytes 524304 | tf_op jit(solution)/shard_map/psum | solution.py:18
  452.5 2.0 log_add_fusion.1
  456.1 27.7 %gather_fusion = f32[8192,32]{1,0:T(8,128)} fusion(f32[32,4096]{0,1:T(8,128)S(1)} %copy.43, s32[8192]{0:T(1024)S(1)} %fusion.12), kind=kCustom, calls=%fused_computation.clone | custom fusion | bytes 2129920 | tf_op jit(solution)/shard_map/jit(_take)/gather | solution.py:36
  483.9 6.5 fusion.8
  490.4 4.0 exponential_reduce_fusion.1
  494.7 77.6 %pmax.14 = f32[32]{0:T(128)S(1)} all-reduce(f32[32]{0:T(128)S(1)} %subtract_reduce_fusion.1), channel_id=1, replica_groups=mesh['traj'=64,'mstate'=4] {'traj','mstate'}, use_global_device_ids=true, to_apply=%region_7.9 | all-reduce | flops 32 | bytes 256 | tf_op jit(solution)/shard_map/pmax | solution.py:40
  572.5 2.7 copy.45
  575.2 44.8 %scatter_custom_fusion.1 = f32[4096,32]{1,0:T(8,128)S(1)} fusion(s32[8192]{0:T(1024)S(1)} %copy-done.10, f32[8192,32]{1,0:T(8,128)} %copy.45, f32[]{:T(128)} %constant.11.clone.1), kind=kCustom, calls=%fused_computation.19 | custom fusion | flops 262144 | bytes 524800 | tf_op jit(solution)/shard_map/scatter-add | solution.py:42
  623.4 248.2 %all-reduce.10.cloned.1.call-done = f32[32,4096]{1,0:T(8,128)} async-done(((f32[32,4096]{1,0:T(8,128)}), f32[32,4096]{1,0:T(8,128)}) %all-reduce.10.cloned.1.call-update) | async-done | bytes 524304 | tf_op jit(solution)/shard_map/psum | solution.py:43
  872.9 6.7 multiply_reduce_fusion
  879.7 176.9 %all-reduce.12.cloned.1.call-done = f32[32,1024]{1,0:T(8,128)} async-done(((f32[32,1024]{1,0:T(8,128)}), f32[32,1024]{1,0:T(8,128)}) %all-reduce.12.cloned.1.call-update) | async-done | bytes 131088 | tf_op jit(solution)/shard_map/psum | solution.py:33
  1057.6 12.1 all_gather.7
  1073.2 27.7 %gather_fusion.1 = f32[8192,32]{1,0:T(8,128)} fusion(f32[32,4096]{0,1:T(8,128)S(1)} %copy.47, s32[8192]{0:T(1024)S(1)} %fusion.12), kind=kCustom, calls=%fused_computation.1.clone | custom fusion | bytes 2129920 | tf_op jit(solution)/shard_map/jit(_take)/gather | solution.py:36
  1100.9 6.5 fusion.9
  1107.5 4.0 exponential_reduce_fusion
  1111.7 74.3 %pmax.15 = f32[32]{0:T(128)S(1)} all-reduce(f32[32]{0:T(128)S(1)} %subtract_reduce_fusion), channel_id=1, replica_groups=mesh['traj'=64,'mstate'=4] {'traj','mstate'}, use_global_device_ids=true, to_apply=%region_15.17 | all-reduce | flops 32 | bytes 256 | tf_op jit(solution)/shard_map/pmax | solution.py:40
  1186.3 2.6 copy.49
  1188.9 45.7 %scatter_custom_fusion.2 = f32[4096,32]{1,0:T(8,128)} fusion(s32[8192]{0:T(1024)S(1)} %copy-done.10, f32[8192,32]{1,0:T(8,128)} %copy.49, f32[]{:T(128)} %constant.11.clone.1), kind=kCustom, calls=%fused_computation.17 | custom fusion | flops 262144 | bytes 524800 | tf_op jit(solution)/shard_map/scatter-add | solution.py:42
  1236.2 255.7 %all-reduce.14.cloned.1.call-done = f32[32,4096]{0,1:T(8,128)} async-done(((f32[32,4096]{0,1:T(8,128)}), f32[32,4096]{0,1:T(8,128)}) %all-reduce.14.cloned.1.call-update) | async-done | bytes 524304 | tf_op jit(solution)/shard_map/psum | solution.py:43
  (59 shorter events, 19.5 us)
Async XLA Ops:
  7.2 188.9 %all-reduce.6.cloned.1.call-start = ((), (), s32[]{:S(2)}) async-start(), calls=%async_computation | async-start | bytes 262144 | tf_op jit(solution)/shard_map/psum | solution.py:33
  9.0 6.7 copy-start.10
  9.0 6.7 copy-start.11
  15.7 50.2 %copy-start.2 = (f32[32,8192]{1,0:T(8,128)S(1)}, f32[32,8192]{1,0:T(8,128)}, u32[]{:S(2)}) copy-start(f32[32,8192]{1,0:T(8,128)} %param.8) | copy-start | bytes 3145732
  15.7 436.8 %all-reduce.8.cloned.1.call-start = ((), (), s32[]{:S(2)}) async-start(), calls=%async_computation.1 | async-start | bytes 1048576 | tf_op jit(solution)/shard_map/psum | solution.py:18
  65.8 386.7 %copy-start.9 = (f32[32,4096]{1,0:T(8,128)S(1)}, f32[32,4096]{1,0:T(8,128)}, u32[]{:S(2)}) copy-start(f32[32,4096]{1,0:T(8,128)} %param.12) | copy-start | bytes 1572868
  65.8 805.8 %all-reduce.10.cloned.1.call-start = ((), (), s32[]{:S(2)}) async-start(), calls=%async_computation.2 | async-start | bytes 1048576 | tf_op jit(solution)/shard_map/psum | solution.py:43
  209.1 243.4 %copy-start.5 = (f32[32,4096]{1,0:T(8,128)}, f32[32,4096]{1,0:T(8,128)S(1)}, u32[]{:S(2)}) copy-start(f32[32,4096]{1,0:T(8,128)S(1)} %all_gather.6) | copy-start | bytes 1572868
  483.9 6.5 copy-start
  483.9 6.5 copy-start.4
  621.5 435.2 %all-reduce.12.cloned.1.call-start = ((), (), s32[]{:S(2)}) async-start(), calls=%async_computation.3 | async-start | bytes 262144 | tf_op jit(solution)/shard_map/psum | solution.py:33
  872.9 197.6 %copy-start.7 = (f32[32,4096]{1,0:T(8,128)S(1)}, f32[32,4096]{1,0:T(8,128)}, u32[]{:S(2)}) copy-start(f32[32,4096]{1,0:T(8,128)} %all-reduce.10.cloned.1.call-done) | copy-start | bytes 1572868
  872.9 197.6 %copy-start.8 = (f32[32,4096]{1,0:T(8,128)S(1)}, f32[32,4096]{1,0:T(8,128)}, u32[]{:S(2)}) copy-start(f32[32,4096]{1,0:T(8,128)} %all-reduce.8.cloned.1.call-done) | copy-start | bytes 1572868
  879.6 612.4 %all-reduce.14.cloned.1.call-start = ((), (), s32[]{:S(2)}) async-start(), calls=%async_computation.4 | async-start | bytes 4194304 | tf_op jit(solution)/shard_map/psum | solution.py:43
  1069.6 0.9 copy-start.6
  1100.9 6.5 copy-start.1
  1100.9 6.5 copy-start.3
Sparse Core Ops, SparseCore 0:
  15.8 180.2 all-reduce.5
  201.5 250.9 all-reduce.7
  621.6 249.9 all-reduce.9
  879.8 176.8 all-reduce.11
  1234.8 257.1 all-reduce.13
where the time goes:
time: 1500 us
  waiting for transfers between devices  1050 us (70%)
  other arithmetic  182 us (12%)
  blocking collectives  176 us (12%)
  local copies, waits for them, and re-layouts  76.4 us (5%)
    psum x2, waiting for transfers between devices, per_device(): total = lax.psum(local_total, ('traj', 'mstate'))  504 us
    psum x2, waiting for transfers between devices, per_device(): row_total = lax.psum(partial_rows, 'traj')  304 us
    psum x1, waiting for transfers between devices, per_device(): visits = lax.psum(local_visits, ('traj', 'mstate'))  243 us
    pmax x2, blocking collectives, per_device(): shift = lax.pmax(jnp.max(term, axis=1), ('traj', 'mstate'))  152 us
    scatter-add x2, other arithmetic, per_device(): local_total = jax.ops.segment_sum(weights.T, labels, num_segments=width).T  90.5 us
    gather x2, local copies, waits for them, and re-layouts, per_device(): scores = jnp.take(level, labels, axis=1) - bias  55.5 us
    scatter-add x1, other arithmetic, per_device(): local_visits = jax.ops.segment_sum(states, labels, num_segments=width).T  48.6 us
  transfers between devices with their start and end apart: 5, of which 5 were waited for; matrix products, arithmetic and copies ran while one was open for 4% of the time, Pallas kernels for 0%

commit v1 on v0

v1 whole, which is shorter than its diff:
```python
import jax
import jax.numpy as jnp
from jax import lax
from jax.sharding import PartitionSpec as P

ITERS = 2


def _xor_pairs(n, bit):
    return [(i, i ^ bit) for i in range(n)]


def _bits(n):
    bit = 1
    while bit < n:
        yield bit
        bit *= 2


def _tree_sum(x, axis, n):
    for bit in _bits(n):
        x = x + lax.ppermute(x, axis, _xor_pairs(n, bit))
    return x


def _lse_merge(top, total, other_top, other_total):
    both = jnp.maximum(top, other_top)
    scaled = total * jnp.exp(top - both)[:, None] + other_total * jnp.exp(other_top - both)[:, None]
    return both, scaled


def _lse_tree(top, total, axis, n):
    for bit in _bits(n):
        other_top, other_total = lax.ppermute((top, total), axis, _xor_pairs(n, bit))
        top, total = _lse_merge(top, total, other_top, other_total)
    return top, total


def _halve(x, axis, n, combine):
    index = lax.axis_index(axis)
    width = x.shape[1]
    bit = n // 2
    while bit >= 1:
        width //= 2
        side = (index // bit) % 2
        keep = lax.dynamic_slice_in_dim(x, side * width, width, 1)
        send = lax.dynamic_slice_in_dim(x, (1 - side) * width, width, 1)
        x = combine(keep, send, bit)
        bit //= 2
    return x


def _sum_halve(x, axis, n):
    return _halve(x, axis, n, lambda keep, send, bit: keep + lax.ppermute(send, axis, _xor_pairs(n, bit)))


def _lse_halve(top, total, axis, n):
    state = {"top": top}

    def combine(keep, send, bit):
        other_top, other = lax.ppermute((state["top"], send), axis, _xor_pairs(n, bit))
        state["top"], merged = _lse_merge(state["top"], keep, other_top, other)
        return merged

    rows = _halve(total, axis, n, combine)
    return state["top"], rows


def _frame_part(level, bias, labels, width):
    scores = jnp.take(level, labels, axis=1) - bias
    top = jnp.max(scores, axis=0)
    logl = top + jnp.log(jnp.sum(jnp.exp(scores - top[None, :]), axis=0))
    term = -bias - logl[None, :]
    local_top = jnp.max(term, axis=1)
    weights = jnp.exp(term - local_top[:, None])
    local_total = jax.ops.segment_sum(weights.T, labels, num_segments=width).T
    return local_top, local_total


def _mult_part(counts_real, free_cols, mult_cols, free_rows, mult_rows):
    weight = jax.nn.sigmoid(
        mult_rows[:, None, :]
        + free_cols[:, :, None]
        - mult_cols[:, :, None]
        - free_rows[:, None, :]
    )
    return jnp.sum(counts_real * weight, axis=1)


def per_device(bias, labels, therm_index, counts, free_start, mult_start):
    n_traj = lax.psum(1, "traj")
    n_mstate = lax.psum(1, "mstate")
    states_k = bias.shape[0]
    width = free_start.shape[1]
    col_count = counts.shape[1]
    row_count = counts.shape[2]
    traj_at = lax.axis_index("traj")
    mstate_at = lax.axis_index("mstate")
    col_start = traj_at * col_count
    row_start = mstate_at * row_count
    per_row = row_count // col_count

    col_pairs = []
    for src_t in range(n_traj):
        for c in range(n_mstate):
            dst_t = c * per_row + src_t // n_mstate
            dst_m = src_t % n_mstate
            col_pairs.append((src_t * n_mstate + c, dst_t * n_mstate + dst_m))
    col_offset = (traj_at // n_mstate) * col_count

    states = jax.nn.one_hot(therm_index, states_k, dtype=jnp.float32)
    local_visits = jax.ops.segment_sum(states, labels, num_segments=width).T
    visits_part = _sum_halve(local_visits, "mstate", n_mstate)
    counts_real = counts.astype(jnp.float32)

    free_cols = lax.dynamic_slice_in_dim(free_start, col_start, col_count, 1)
    mult_cols = lax.dynamic_slice_in_dim(mult_start, col_start, col_count, 1)
    free_rows = lax.dynamic_slice_in_dim(free_start, row_start, row_count, 1)
    mult_rows = lax.dynamic_slice_in_dim(mult_start, row_start, row_count, 1)
    visits_rows = None
    for step in range(ITERS):
        partial_rows = _mult_part(counts_real, free_cols, mult_cols, free_rows, mult_rows)
        if step == 0:
            both = _tree_sum(jnp.concatenate([partial_rows, visits_part], axis=1), "traj", n_traj)
            row_total, visits_rows = both[:, :row_count], both[:, row_count:]
        else:
            row_total = _tree_sum(partial_rows, "traj", n_traj)
        mult_rows = jnp.log(0.5 + row_total)
        level_rows = jnp.log(jnp.exp(mult_rows) + visits_rows) + free_rows
        level = lax.all_gather(level_rows, "mstate", axis=1, tiled=True)
        local_top, local_total = _frame_part(level, bias, labels, width)
        top, total = _lse_halve(local_top, local_total, "mstate", n_mstate)
        top, total = _lse_tree(top, total, "traj", n_traj)
        free_rows = -(top[:, None] + jnp.log(total))
        if step + 1 < ITERS:
            block = jnp.stack([
                lax.dynamic_slice_in_dim(free_rows, col_offset, col_count, 1),
                lax.dynamic_slice_in_dim(mult_rows, col_offset, col_count, 1),
            ])
            block = lax.ppermute(block, ("traj", "mstate"), col_pairs)
            free_cols, mult_cols = block[0], block[1]
    return (free_rows, mult_rows)


def solution(mesh):
    placed = (
        P(None, ("traj", "mstate")),
        P(("traj", "mstate")),
        P(("traj", "mstate")),
        P(None, "traj", "mstate"),
        P(),
        P(),
    )
    return jax.shard_map(
        per_device,
        mesh=mesh,
        in_specs=placed,
        out_specs=(P(None, "mstate"), P(None, "mstate")),
        check_vma=False,
    )
```

time: 1500 us -> 573 us (0.38)
  waiting for transfers between devices: 1050 us -> 169 us
  blocking collectives: 176 us -> 24 us
  starting transfers between devices: 0.39 us -> 116 us
    psum x5 -> x0, waiting for transfers between devices: 1050 us -> none  [the longest x2 504 us: per_device(): total = lax.psum(local_total, ('traj', 'mstate'))]
    ppermute x0 -> x47, waiting for transfers between devices: none -> 169 us  [the longest x24 92.7 us: _lse_tree(): lax.ppermute((top, total), axis, _xor_pairs(n, bit))]
    pmax x2 -> x0, blocking collectives: 152 us -> none  [per_device(): shift = lax.pmax(jnp.max(term, axis=1), ('traj', 'mstate'))]
    ppermute x0 -> x47, starting transfers between devices: none -> 116 us  [the longest x24 56.6 us: _lse_tree(): lax.ppermute((top, total), axis, _xor_pairs(n, bit))]
  transfers between devices with their start and end apart: 5 -> 47, of which waited for: 5 -> 31; matrix products, arithmetic and copies ran while one was open for 4% -> 20% of each run, Pallas kernels for 0% -> 0%
where the time goes in v1:
time: 573 us; the launch traced here: 564 us
  other arithmetic  171 us (30%)
  waiting for transfers between devices  169 us (29%)
  starting transfers between devices  116 us (20%)
  local copies, waits for them, and re-layouts  82 us (14%)
  blocking collectives  24 us (4%)
    ppermute x24, waiting for transfers between devices, _lse_tree(): lax.ppermute((top, total), axis, _xor_pairs(n, bit))  92.7 us
    scatter-add x2, other arithmetic, _frame_part(): local_total = jax.ops.segment_sum(weights.T, labels, num_segments=width).T  89.6 us
    gather x2, local copies, waits for them, and re-layouts, _frame_part(): scores = jnp.take(level, labels, axis=1) - bias  58.6 us
    ppermute x24, starting transfers between devices, _lse_tree(): lax.ppermute((top, total), axis, _xor_pairs(n, bit))  56.6 us
    ppermute x12, waiting for transfers between devices, _tree_sum(): x = x + lax.ppermute(x, axis, _xor_pairs(n, bit))  52.2 us
    scatter-add x1, other arithmetic, per_device(): local_visits = jax.ops.segment_sum(states, labels, num_segments=width).T  44 us
    ppermute x12, starting transfers between devices, _tree_sum(): x = x + lax.ppermute(x, axis, _xor_pairs(n, bit))  34.3 us
    all_gather x2, blocking collectives, per_device(): level = lax.all_gather(level_rows, 'mstate', axis=1, tiled=True)  24 us
  transfers between devices with their start and end apart: 47, of which 31 were waited for; matrix products, arithmetic and copies ran while one was open for 20% of the time, Pallas kernels for 0%

profile of v1, /device:TPU:1, one launch (start us, length us, event | category | flops | bytes accessed | tf_op | source)
XLA Modules:
  0.0 563.9 jit_solution(4422621257494549277)
XLA Ops:
  0.7 44.0 %scatter_custom_fusion = f32[4096,32]{1,0:T(8,128)S(1)} fusion(s32[8192]{0:T(1024)} %param.9, s32[8192]{0:T(1024)} %param.10, f32[]{:T(128)} %constant.92.clone.1), kind=kCustom, calls=%fused_computation.11 | custom fusion | flops 786432 | bytes 557568 | tf_op jit(solution)/shard_map/scatter-add | solution.py:112
  58.3 6.0 %multiply_reduce_fusion.1 = f32[32,1024]{1,0:T(8,128)S(1)} fusion(s32[32,64,1024]{2,1,0:T(8,128)} %param.11, f32[32,1024]{1,0:T(8,128)S(1)} %get-tuple-element.73, f32[32,64]{1,0:T(8,128)S(1)} %get-tuple-element.75, f32[32,64]{1,0:T(8,128)S(1)} %get-tuple-element.76, f32[32,1024]{1,0:T(8,128)S(1)} %get-tuple-element.74), kind=kLoop, calls=%fused_computation.6 | loop fusion | flops 18841600 | bytes 8798208 | tf_op jit(solution)/shard_map/reduce_sum | solution.py:87
  68.9 6.2 %collective-permute-done.3 = f32[32,2048]{1,0:T(8,128)S(1)} collective-permute-done((f32[32,2048]{1,0:T(8,128)S(1)}, f32[32,2048]{1,0:T(8,128)S(1)}, u32[]{:S(2)}, u32[]{:S(2)}) %collective-permute-start.3) | collective-permute-done | bytes 262176 | tf_op jit(solution)/shard_map/ppermute | solution.py:22
  92.7 11.4 %collective-permute-done.6 = f32[32,2048]{1,0:T(8,128)S(1)} collective-permute-done((f32[32,2048]{1,0:T(8,128)S(1)}, f32[32,2048]{1,0:T(8,128)S(1)}, u32[]{:S(2)}, u32[]{:S(2)}) %collective-permute-start.6) | collective-permute-done | bytes 262176 | tf_op jit(solution)/shard_map/ppermute | solution.py:22
  104.1 6.5 %collective-permute-start.7 = (f32[32,2048]{1,0:T(8,128)S(1)}, f32[32,2048]{1,0:T(8,128)S(1)}, u32[]{:S(2)}, u32[]{:S(2)}) collective-permute-start(f32[32,2048]{1,0:T(8,128)S(1)} %add.248), channel_id=1, source_target_pairs={{0,128},{4,132},{8,136},{12,140},{16,144},{20,148},{24,152},{28,15... | collective-permute-start | bytes 786440 | tf_op jit(solution)/shard_map/ppermute | solution.py:22
  119.4 10.9 %all_gather.6 = f32[32,4096]{1,0:T(8,128)} all-gather(f32[32,1024]{1,0:T(8,128)S(1)} %get-tuple-element.56), channel_id=1, replica_groups=mesh['traj'=64,'mstate'=4] {'mstate'}, dimensions={1}, use_global_device_ids=true | all-gather | bytes 655360 | tf_op jit(solution)/shard_map/all_gather | solution.py:130
  131.9 30.6 %gather_fusion = f32[8192,32]{1,0:T(8,128)} fusion(f32[32,4096]{0,1:T(8,128)S(1)} %copy.121, s32[8192]{0:T(1024)} %fusion.11), kind=kCustom, calls=%fused_computation.clone | custom fusion | bytes 2129920 | tf_op jit(solution)/shard_map/jit(_take)/gather | solution.py:70
  162.5 6.5 %fusion.8 = f32[8192]{0:T(1024)S(1)} fusion(f32[32,8192]{0,1:T(8,128)} %copy.122, f32[8192,32]{1,0:T(8,128)} %gather_fusion, pred[8192]{0:T(1024)(128)(4,1)S(1)} %compare_and_fusion), kind=kLoop, calls=%fused_computation.28 | loop fusion | flops 778240 | bytes 2138112 | tf_op jit(solution)/shard_map/reduce_max | solution.py:71
  177.6 44.8 %scatter_custom_fusion.1 = f32[4096,32]{1,0:T(8,128)S(1)} fusion(s32[8192]{0:T(1024)} %param.9, f32[8192,32]{1,0:T(8,128)} %copy.123, f32[]{:T(128)} %constant.92.clone.1), kind=kCustom, calls=%fused_computation.23 | custom fusion | flops 262144 | bytes 524800 | tf_op jit(solution)/shard_map/scatter-add | solution.py:76
  231.6 8.7 %collective-permute-start.10 = (f32[32]{0:T(128)S(1)}, f32[32]{0:T(128)S(1)}, u32[]{:S(2)}, u32[]{:S(2)}) collective-permute-start(f32[32]{0:T(128)S(1)} %get-tuple-element.48), channel_id=1, source_target_pairs={{0,4},{4,0},{8,12},{12,8},{16,20},{20,16},{24,28},{28,24},{32,36},... | collective-permute-start | bytes 392 | tf_op jit(solution)/shard_map/ppermute | solution.py:34
  278.7 9.9 %collective-permute-start.24 = (f32[2,32,64]{2,1,0:T(8,128)S(1)}, f32[2,32,64]{2,1,0:T(8,128)S(1)}, u32[]{:S(2)}, u32[]{:S(2)}) collective-permute-start(f32[2,32,64]{2,1,0:T(8,128)S(1)} %pad_maximum_fusion.1), channel_id=1, source_target_pairs={{0,0},{1,64},{2,128},{3,192},{4,1},{5,65},{6,129},{7,193},{8,2},{9... | collective-permute-start | bytes 49160 | tf_op jit(solution)/shard_map/ppermute | solution.py:140
  290.4 6.0 %multiply_reduce_fusion = f32[32,1024]{1,0:T(8,128)S(1)} fusion(s32[32,64,1024]{2,1,0:T(8,128)} %param.11, f32[32,1024]{1,0:T(8,128)S(1)} %add_negate_fusion.1, f32[32,64]{1,0:T(8,128)S(1)} %get-tuple-element.58, f32[32,64]{1,0:T(8,128)S(1)} %get-tuple-element.57, f32[32,1024]{1,0:T(8,128)S(1)} %get-tuple-element.55), kind=kLoop, calls=%fused_computation.5 | loop fusion | flops 18841600 | bytes 8798208 | tf_op jit(solution)/shard_map/reduce_sum | solution.py:87
  304.0 6.4 %collective-permute-start.27 = (f32[32,1024]{1,0:T(8,128)S(1)}, f32[32,1024]{1,0:T(8,128)S(1)}, u32[]{:S(2)}, u32[]{:S(2)}) collective-permute-start(f32[32,1024]{1,0:T(8,128)S(1)} %add.271), channel_id=1, source_target_pairs={{0,16},{4,20},{8,24},{12,28},{16,0},{20,4},{24,8},{28,12},{32,48},... | collective-permute-start | bytes 393224 | tf_op jit(solution)/shard_map/ppermute | solution.py:22
  332.3 13.1 %all_gather.7 = f32[32,4096]{1,0:T(8,128)} all-gather(f32[32,1024]{1,0:T(8,128)S(1)} %get-tuple-element.33), channel_id=1, replica_groups=mesh['traj'=64,'mstate'=4] {'mstate'}, dimensions={1}, use_global_device_ids=true | all-gather | bytes 655360 | tf_op jit(solution)/shard_map/all_gather | solution.py:130
  347.1 28.0 %gather_fusion.1 = f32[8192,32]{1,0:T(8,128)} fusion(f32[32,4096]{0,1:T(8,128)S(1)} %copy.126, s32[8192]{0:T(1024)S(1)} %copy-done.5), kind=kCustom, calls=%fused_computation.1.clone | custom fusion | bytes 2129920 | tf_op jit(solution)/shard_map/jit(_take)/gather | solution.py:70
  375.1 6.5 %fusion.9 = f32[8192]{0:T(1024)S(1)} fusion(f32[32,8192]{0,1:T(8,128)} %copy.122, f32[8192,32]{1,0:T(8,128)} %gather_fusion.1, pred[8192]{0:T(1024)(128)(4,1)S(1)} %compare_and_fusion), kind=kLoop, calls=%fused_computation.29 | loop fusion | flops 778240 | bytes 2138112 | tf_op jit(solution)/shard_map/reduce_max | solution.py:71
  390.3 44.8 %scatter_custom_fusion.2 = f32[4096,32]{1,0:T(8,128)S(1)} fusion(s32[8192]{0:T(1024)} %param.9, f32[8192,32]{1,0:T(8,128)} %copy.128, f32[]{:T(128)} %constant.92.clone.1), kind=kCustom, calls=%fused_computation.21 | custom fusion | flops 262144 | bytes 524800 | tf_op jit(solution)/shard_map/scatter-add | solution.py:76
  441.5 9.3 %collective-permute-start.33 = (f32[32]{0:T(128)S(1)}, f32[32]{0:T(128)S(1)}, u32[]{:S(2)}, u32[]{:S(2)}) collective-permute-start(f32[32]{0:T(128)S(1)} %get-tuple-element.30), channel_id=1, source_target_pairs={{0,4},{4,0},{8,12},{12,8},{16,20},{20,16},{24,28},{28,24},{32,36},... | collective-permute-start | bytes 392 | tf_op jit(solution)/shard_map/ppermute | solution.py:34
  453.6 11.5 %collective-permute-done.40 = f32[32,1024]{0,1:T(8,128)S(1)} collective-permute-done((f32[32,1024]{0,1:T(8,128)S(1)}, f32[32,1024]{0,1:T(8,128)S(1)}, u32[]{:S(2)}, u32[]{:S(2)}) %collective-permute-start.40) | collective-permute-done | bytes 131104 | tf_op jit(solution)/shard_map/ppermute | solution.py:61
  471.4 11.3 %collective-permute-done.42 = f32[32,1024]{0,1:T(8,128)S(1)} collective-permute-done((f32[32,1024]{0,1:T(8,128)S(1)}, f32[32,1024]{0,1:T(8,128)S(1)}, u32[]{:S(2)}, u32[]{:S(2)}) %collective-permute-start.42) | collective-permute-done | bytes 131104 | tf_op jit(solution)/shard_map/ppermute | solution.py:34
  486.7 10.1 %collective-permute-done.43 = f32[32,1024]{0,1:T(8,128)S(1)} collective-permute-done((f32[32,1024]{0,1:T(8,128)S(1)}, f32[32,1024]{0,1:T(8,128)S(1)}, u32[]{:S(2)}, u32[]{:S(2)}) %collective-permute-start.43) | collective-permute-done | bytes 131104 | tf_op jit(solution)/shard_map/ppermute | solution.py:34
  500.3 8.5 %collective-permute-done.44 = f32[32,1024]{0,1:T(8,128)S(1)} collective-permute-done((f32[32,1024]{0,1:T(8,128)S(1)}, f32[32,1024]{0,1:T(8,128)S(1)}, u32[]{:S(2)}, u32[]{:S(2)}) %collective-permute-start.44) | collective-permute-done | bytes 131104 | tf_op jit(solution)/shard_map/ppermute | solution.py:34
  511.3 22.7 %collective-permute-done.45 = f32[32,1024]{0,1:T(8,128)S(1)} collective-permute-done((f32[32,1024]{0,1:T(8,128)S(1)}, f32[32,1024]{0,1:T(8,128)S(1)}, u32[]{:S(2)}, u32[]{:S(2)}) %collective-permute-start.45) | collective-permute-done | bytes 131104 | tf_op jit(solution)/shard_map/ppermute | solution.py:34
  538.0 24.5 %collective-permute-done.46 = f32[32,1024]{0,1:T(8,128)S(1)} collective-permute-done((f32[32,1024]{0,1:T(8,128)S(1)}, f32[32,1024]{0,1:T(8,128)S(1)}, u32[]{:S(2)}, u32[]{:S(2)}) %collective-permute-start.46) | collective-permute-done | bytes 131104 | tf_op jit(solution)/shard_map/ppermute | solution.py:34
  (179 shorter events, 173.8 us)
Async XLA Ops:
  47.4 8.6 %collective-permute-start = (f32[32,2048]{1,0:T(8,128)S(1)}, f32[32,2048]{1,0:T(8,128)S(1)}, u32[]{:S(2)}, u32[]{:S(2)}) collective-permute-start(f32[32,2048]{1,0:T(8,128)S(1)} %copy.120), channel_id=1, source_target_pairs={{0,2},{1,3},{2,0},{3,1},{4,6},{5,7},{6,4},{7,5},{8,10},{9,11},{10,... | collective-permute-start | bytes 786440 | tf_op jit(solution)/shard_map/ppermute | solution.py:54
  56.1 8.3 %collective-permute-start.1 = (f32[32,1024]{1,0:T(8,128)S(1)}, f32[32,1024]{1,0:T(8,128)S(1)}, u32[]{:S(2)}, u32[]{:S(2)}) collective-permute-start(f32[32,1024]{1,0:T(8,128)S(1)} %constant_dynamic-slice_fusion.3), channel_id=1, source_target_pairs={{0,1},{1,0},{2,3},{3,2},{4,5},{5,4},{6,7},{7,6},{8,9},{9,8},{10,11... | collective-permute-start | bytes 393224 | tf_op jit(solution)/shard_map/ppermute | solution.py:54
  75.1 8.2 %collective-permute-start.4 = (f32[32,2048]{1,0:T(8,128)S(1)}, f32[32,2048]{1,0:T(8,128)S(1)}, u32[]{:S(2)}, u32[]{:S(2)}) collective-permute-start(f32[32,2048]{1,0:T(8,128)S(1)} %add.245), channel_id=1, source_target_pairs={{0,16},{4,20},{8,24},{12,28},{16,0},{20,4},{24,8},{28,12},{32,48},... | collective-permute-start | bytes 786440 | tf_op jit(solution)/shard_map/ppermute | solution.py:22
  89.6 14.4 %collective-permute-start.6 = (f32[32,2048]{1,0:T(8,128)S(1)}, f32[32,2048]{1,0:T(8,128)S(1)}, u32[]{:S(2)}, u32[]{:S(2)}) collective-permute-start(f32[32,2048]{1,0:T(8,128)S(1)} %add.247), channel_id=1, source_target_pairs={{0,64},{4,68},{8,72},{12,76},{16,80},{20,84},{24,88},{28,92},{32,9... | collective-permute-start | bytes 786440 | tf_op jit(solution)/shard_map/ppermute | solution.py:22
  104.1 15.2 %collective-permute-start.7 = (f32[32,2048]{1,0:T(8,128)S(1)}, f32[32,2048]{1,0:T(8,128)S(1)}, u32[]{:S(2)}, u32[]{:S(2)}) collective-permute-start(f32[32,2048]{1,0:T(8,128)S(1)} %add.248), channel_id=1, source_target_pairs={{0,128},{4,132},{8,136},{12,140},{16,144},{20,148},{24,152},{28,15... | collective-permute-start | bytes 786440 | tf_op jit(solution)/shard_map/ppermute | solution.py:22
  173.6 53.8 %collective-permute-start.8 = (f32[32]{0:T(128)S(1)}, f32[32]{0:T(128)S(1)}, u32[]{:S(2)}, u32[]{:S(2)}) collective-permute-start(f32[32]{0:T(128)S(1)} %subtract_reduce_fusion.1), channel_id=1, source_target_pairs={{0,2},{1,3},{2,0},{3,1},{4,6},{5,7},{6,4},{7,5},{8,10},{9,11},{10,... | collective-permute-start | bytes 392 | tf_op jit(solution)/shard_map/ppermute | solution.py:61
  225.5 14.8 %collective-permute-start.16 = (f32[32,2048]{1,0:T(8,128)S(1)}, f32[32,2048]{1,0:T(8,128)S(1)}, u32[]{:S(2)}, u32[]{:S(2)}) collective-permute-start(f32[32,2048]{1,0:T(8,128)S(1)} %copy.125), channel_id=1, source_target_pairs={{0,2},{1,3},{2,0},{3,1},{4,6},{5,7},{6,4},{7,5},{8,10},{9,11},{10,... | collective-permute-start | bytes 786440 | tf_op jit(solution)/shard_map/ppermute | solution.py:61
  231.6 9.9 %collective-permute-start.10 = (f32[32]{0:T(128)S(1)}, f32[32]{0:T(128)S(1)}, u32[]{:S(2)}, u32[]{:S(2)}) collective-permute-start(f32[32]{0:T(128)S(1)} %get-tuple-element.48), channel_id=1, source_target_pairs={{0,4},{4,0},{8,12},{12,8},{16,20},{20,16},{24,28},{28,24},{32,36},... | collective-permute-start | bytes 392 | tf_op jit(solution)/shard_map/ppermute | solution.py:34
  270.7 7.8 %collective-permute-start.23 = (f32[32,1024]{1,0:T(8,128)S(1)}, f32[32,1024]{1,0:T(8,128)S(1)}, u32[]{:S(2)}, u32[]{:S(2)}) collective-permute-start(f32[32,1024]{1,0:T(8,128)S(1)} %multiply_add_fusion.6), channel_id=1, source_target_pairs={{0,128},{4,132},{8,136},{12,140},{16,144},{20,148},{24,152},{28,15... | collective-permute-start | bytes 393224 | tf_op jit(solution)/shard_map/ppermute | solution.py:34
  278.7 11.7 %collective-permute-start.24 = (f32[2,32,64]{2,1,0:T(8,128)S(1)}, f32[2,32,64]{2,1,0:T(8,128)S(1)}, u32[]{:S(2)}, u32[]{:S(2)}) collective-permute-start(f32[2,32,64]{2,1,0:T(8,128)S(1)} %pad_maximum_fusion.1), channel_id=1, source_target_pairs={{0,0},{1,64},{2,128},{3,192},{4,1},{5,65},{6,129},{7,193},{8,2},{9... | collective-permute-start | bytes 49160 | tf_op jit(solution)/shard_map/ppermute | solution.py:140
  304.0 9.1 %collective-permute-start.27 = (f32[32,1024]{1,0:T(8,128)S(1)}, f32[32,1024]{1,0:T(8,128)S(1)}, u32[]{:S(2)}, u32[]{:S(2)}) collective-permute-start(f32[32,1024]{1,0:T(8,128)S(1)} %add.271), channel_id=1, source_target_pairs={{0,16},{4,20},{8,24},{12,28},{16,0},{20,4},{24,8},{28,12},{32,48},... | collective-permute-start | bytes 393224 | tf_op jit(solution)/shard_map/ppermute | solution.py:22
  386.1 51.2 %collective-permute-start.31 = (f32[32]{0:T(128)S(1)}, f32[32]{0:T(128)S(1)}, u32[]{:S(2)}, u32[]{:S(2)}) collective-permute-start(f32[32]{0:T(128)S(1)} %subtract_reduce_fusion), channel_id=1, source_target_pairs={{0,2},{1,3},{2,0},{3,1},{4,6},{5,7},{6,4},{7,5},{8,10},{9,11},{10,... | collective-permute-start | bytes 392 | tf_op jit(solution)/shard_map/ppermute | solution.py:61
  435.5 15.3 %collective-permute-start.39 = (f32[32,2048]{1,0:T(8,128)S(1)}, f32[32,2048]{1,0:T(8,128)}, u32[]{:S(2)}, u32[]{:S(2)}) collective-permute-start(f32[32,2048]{1,0:T(8,128)S(1)} %copy.129), channel_id=1, source_target_pairs={{0,2},{1,3},{2,0},{3,1},{4,6},{5,7},{6,4},{7,5},{8,10},{9,11},{10,... | collective-permute-start | bytes 786440 | tf_op jit(solution)/shard_map/ppermute | solution.py:61
  441.5 11.9 %collective-permute-start.33 = (f32[32]{0:T(128)S(1)}, f32[32]{0:T(128)S(1)}, u32[]{:S(2)}, u32[]{:S(2)}) collective-permute-start(f32[32]{0:T(128)S(1)} %get-tuple-element.30), channel_id=1, source_target_pairs={{0,4},{4,0},{8,12},{12,8},{16,20},{20,16},{24,28},{28,24},{32,36},... | collective-permute-start | bytes 392 | tf_op jit(solution)/shard_map/ppermute | solution.py:34
  452.3 12.9 %collective-permute-start.40 = (f32[32,1024]{0,1:T(8,128)S(1)}, f32[32,1024]{0,1:T(8,128)S(1)}, u32[]{:S(2)}, u32[]{:S(2)}) collective-permute-start(f32[32,1024]{0,1:T(8,128)S(1)} %constant_dynamic-slice_fusion), channel_id=1, source_target_pairs={{0,1},{1,0},{2,3},{3,2},{4,5},{5,4},{6,7},{7,6},{8,9},{9,8},{10,11... | collective-permute-start | bytes 393224 | tf_op jit(solution)/shard_map/ppermute | solution.py:61
  453.4 13.5 %collective-permute-start.34 = (f32[32]{0:T(128)S(1)}, f32[32]{0:T(128)S(1)}, u32[]{:S(2)}, u32[]{:S(2)}) collective-permute-start(f32[32]{0:T(128)S(1)} %get-tuple-element.28), channel_id=1, source_target_pairs={{0,8},{4,12},{8,0},{12,4},{16,24},{20,28},{24,16},{28,20},{32,40},... | collective-permute-start | bytes 392 | tf_op jit(solution)/shard_map/ppermute | solution.py:34
  468.9 13.7 %collective-permute-start.42 = (f32[32,1024]{0,1:T(8,128)S(1)}, f32[32,1024]{0,1:T(8,128)S(1)}, u32[]{:S(2)}, u32[]{:S(2)}) collective-permute-start(f32[32,1024]{0,1:T(8,128)S(1)} %multiply_add_fusion.4), channel_id=1, source_target_pairs={{0,8},{4,12},{8,0},{12,4},{16,24},{20,28},{24,16},{28,20},{32,40},... | collective-permute-start | bytes 393224 | tf_op jit(solution)/shard_map/ppermute | solution.py:34
  470.9 13.9 %collective-permute-start.36 = (f32[32]{0:T(128)S(1)}, f32[32]{0:T(128)S(1)}, u32[]{:S(2)}, u32[]{:S(2)}) collective-permute-start(f32[32]{0:T(128)S(1)} %get-tuple-element.24), channel_id=1, source_target_pairs={{0,32},{4,36},{8,40},{12,44},{16,48},{20,52},{24,56},{28,60},{32,0... | collective-permute-start | bytes 392 | tf_op jit(solution)/shard_map/ppermute | solution.py:34
  482.7 14.2 %collective-permute-start.43 = (f32[32,1024]{0,1:T(8,128)S(1)}, f32[32,1024]{0,1:T(8,128)S(1)}, u32[]{:S(2)}, u32[]{:S(2)}) collective-permute-start(f32[32,1024]{0,1:T(8,128)S(1)} %multiply_add_fusion.3), channel_id=1, source_target_pairs={{0,16},{4,20},{8,24},{12,28},{16,0},{20,4},{24,8},{28,12},{32,48},... | collective-permute-start | bytes 393224 | tf_op jit(solution)/shard_map/ppermute | solution.py:34
  484.8 12.9 %collective-permute-start.37 = (f32[32]{0:T(128)S(1)}, f32[32]{0:T(128)S(1)}, u32[]{:S(2)}, u32[]{:S(2)}) collective-permute-start(f32[32]{0:T(128)S(1)} %get-tuple-element.22), channel_id=1, source_target_pairs={{0,64},{4,68},{8,72},{12,76},{16,80},{20,84},{24,88},{28,92},{32,9... | collective-permute-start | bytes 392 | tf_op jit(solution)/shard_map/ppermute | solution.py:34
  497.0 11.8 %collective-permute-start.44 = (f32[32,1024]{0,1:T(8,128)S(1)}, f32[32,1024]{0,1:T(8,128)S(1)}, u32[]{:S(2)}, u32[]{:S(2)}) collective-permute-start(f32[32,1024]{0,1:T(8,128)S(1)} %multiply_add_fusion.2), channel_id=1, source_target_pairs={{0,32},{4,36},{8,40},{12,44},{16,48},{20,52},{24,56},{28,60},{32,0... | collective-permute-start | bytes 393224 | tf_op jit(solution)/shard_map/ppermute | solution.py:34
  497.7 13.5 %collective-permute-start.38 = (f32[32]{0:T(128)S(1)}, f32[32]{0:T(128)S(1)}, u32[]{:S(2)}, u32[]{:S(2)}) collective-permute-start(f32[32]{0:T(128)S(1)} %get-tuple-element.20), channel_id=1, source_target_pairs={{0,128},{4,132},{8,136},{12,140},{16,144},{20,148},{24,152},{28,15... | collective-permute-start | bytes 392 | tf_op jit(solution)/shard_map/ppermute | solution.py:34
  508.8 25.2 %collective-permute-start.45 = (f32[32,1024]{0,1:T(8,128)S(1)}, f32[32,1024]{0,1:T(8,128)S(1)}, u32[]{:S(2)}, u32[]{:S(2)}) collective-permute-start(f32[32,1024]{0,1:T(8,128)S(1)} %multiply_add_fusion.1), channel_id=1, source_target_pairs={{0,64},{4,68},{8,72},{12,76},{16,80},{20,84},{24,88},{28,92},{32,9... | collective-permute-start | bytes 393224 | tf_op jit(solution)/shard_map/ppermute | solution.py:34
  534.1 28.4 %collective-permute-start.46 = (f32[32,1024]{0,1:T(8,128)S(1)}, f32[32,1024]{0,1:T(8,128)S(1)}, u32[]{:S(2)}, u32[]{:S(2)}) collective-permute-start(f32[32,1024]{0,1:T(8,128)S(1)} %multiply_add_fusion), channel_id=1, source_target_pairs={{0,128},{4,132},{8,136},{12,140},{16,144},{20,148},{24,152},{28,15... | collective-permute-start | bytes 393224 | tf_op jit(solution)/shard_map/ppermute | solution.py:34
  (30 other events, 283.5 us)

commit v2 on v1

--- a/solution.py
+++ b/solution.py
@@ -10,60 +10,53 @@
     return [(i, i ^ bit) for i in range(n)]
 
 
-def _bits(n):
-    bit = 1
-    while bit < n:
-        yield bit
-        bit *= 2
+def _add(a, b):
+    return a + b
 
 
-def _tree_sum(x, axis, n):
-    for bit in _bits(n):
-        x = x + lax.ppermute(x, axis, _xor_pairs(n, bit))
+def _lse_merge(a, b):
+    top = jnp.maximum(a[:, -1:], b[:, -1:])
+    body = a[:, :-1] * jnp.exp(a[:, -1:] - top) + b[:, :-1] * jnp.exp(b[:, -1:] - top)
+    return jnp.concatenate([body, top], axis=1)
+
+
+def _tree(x, axis, n, merge):
+    shift = 1
+    while shift < n:
+        wide = 4 if shift * 4 <= n else 2
+        got = [lax.ppermute(x, axis, _xor_pairs(n, j * shift)) for j in range(1, wide)]
+        if wide == 4:
+            x = merge(merge(x, got[0]), merge(got[1], got[2]))
+        else:
+            x = merge(x, got[0])
+        shift *= wide
     return x
 
 
-def _lse_merge(top, total, other_top, other_total):
-    both = jnp.maximum(top, other_top)
-    scaled = total * jnp.exp(top - both)[:, None] + other_total * jnp.exp(other_top - both)[:, None]
-    return both, scaled
+def _scatter_blocks(x, axis, n, merge, extra=None):
+    index = lax.axis_index(axis)
+    width = x.shape[1] // n
+
+    def block(b):
+        piece = lax.dynamic_slice_in_dim(x, b * width, width, 1)
+        return piece if extra is None else jnp.concatenate([piece, extra], axis=1)
+
+    own = block(index)
+    got = [lax.ppermute(block(index ^ j), axis, _xor_pairs(n, j)) for j in range(1, n)]
+    while got:
+        own = merge(own, got.pop(0))
+    return own
 
 
-def _lse_tree(top, total, axis, n):
-    for bit in _bits(n):
-        other_top, other_total = lax.ppermute((top, total), axis, _xor_pairs(n, bit))
-        top, total = _lse_merge(top, total, other_top, other_total)
-    return top, total
-
-
-def _halve(x, axis, n, combine):
+def _gather_blocks(x, axis, n):
     index = lax.axis_index(axis)
     width = x.shape[1]
-    bit = n // 2
-    while bit >= 1:
-        width //= 2
-        side = (index // bit) % 2
-        keep = lax.dynamic_slice_in_dim(x, side * width, width, 1)
-        send = lax.dynamic_slice_in_dim(x, (1 - side) * width, width, 1)
-        x = combine(keep, send, bit)
-        bit //= 2
-    return x
-
-
-def _sum_halve(x, axis, n):
-    return _halve(x, axis, n, lambda keep, send, bit: keep + lax.ppermute(send, axis, _xor_pairs(n, bit)))
-
-
-def _lse_halve(top, total, axis, n):
-    state = {"top": top}
-
-    def combine(keep, send, bit):
-        other_top, other = lax.ppermute((state["top"], send), axis, _xor_pairs(n, bit))
-        state["top"], merged = _lse_merge(state["top"], keep, other_top, other)
-        return merged
-
-    rows = _halve(total, axis, n, combine)
-    return state["top"], rows
+    full = jnp.zeros((x.shape[0], width * n), x.dtype)
+    full = lax.dynamic_update_slice_in_dim(full, x, index * width, 1)
+    for j in range(1, n):
+        got = lax.ppermute(x, axis, _xor_pairs(n, j))
+        full = lax.dynamic_update_slice_in_dim(full, got, (index ^ j) * width, 1)
+    return full
 
 
 def _frame_part(level, bias, labels, width):
@@ -110,7 +103,7 @@
 
     states = jax.nn.one_hot(therm_index, states_k, dtype=jnp.float32)
     local_visits = jax.ops.segment_sum(states, labels, num_segments=width).T
-    visits_part = _sum_halve(local_visits, "mstate", n_mstate)
+    visits_part = _scatter_blocks(local_visits, "mstate", n_mstate, _add)
     counts_real = counts.astype(jnp.float32)
 
     free_cols = lax.dynamic_slice_in_dim(free_start, col_start, col_count, 1)
@@ -121,17 +114,17 @@
     for step in range(ITERS):
         partial_rows = _mult_part(counts_real, free_cols, mult_cols, free_rows, mult_rows)
         if step == 0:
-            both = _tree_sum(jnp.concatenate([partial_rows, visits_part], axis=1), "traj", n_traj)
+            both = _tree(jnp.concatenate([partial_rows, visits_part], axis=1), "traj", n_traj, _add)
             row_total, visits_rows = both[:, :row_count], both[:, row_count:]
         else:
-            row_total = _tree_sum(partial_rows, "traj", n_traj)
+            row_total = _tree(partial_rows, "traj", n_traj, _add)
         mult_rows = jnp.log(0.5 + row_total)
         level_rows = jnp.log(jnp.exp(mult_rows) + visits_rows) + free_rows
-        level = lax.all_gather(level_rows, "mstate", axis=1, tiled=True)
+        level = _gather_blocks(level_rows, "mstate", n_mstate)
         local_top, local_total = _frame_part(level, bias, labels, width)
-        top, total = _lse_halve(local_top, local_total, "mstate", n_mstate)
-        top, total = _lse_tree(top, total, "traj", n_traj)
-        free_rows = -(top[:, None] + jnp.log(total))
+        packed = _scatter_blocks(local_total, "mstate", n_mstate, _lse_merge, local_top[:, None])
+        packed = _tree(packed, "traj", n_traj, _lse_merge)
+        free_rows = -(packed[:, -1:] + jnp.log(packed[:, :-1]))
         if step + 1 < ITERS:
             block = jnp.stack([
                 lax.dynamic_slice_in_dim(free_rows, col_offset, col_count, 1),

time: 573 us -> 517 us (0.902)
  waiting for transfers between devices: 169 us -> 138 us
  starting transfers between devices: 116 us -> 88.1 us
  local copies, waits for them, and re-layouts: 82 us -> 108 us
  blocking collectives: 24 us -> 0 us
    ppermute x46 -> x51, waiting for transfers between devices: 167 us -> 133 us  [the longest x36 120 us: _tree(): lax.ppermute(x, axis, _xor_pairs(n, j * shift))]
    all_gather x2 -> x0, blocking collectives: 24 us -> none  [per_device(): level = lax.all_gather(level_rows, 'mstate', axis=1, tiled=True)]
    ppermute x46 -> x51, starting transfers between devices: 106 us -> 85.7 us  [the longest x36 65.2 us: _tree(): lax.ppermute(x, axis, _xor_pairs(n, j * shift))]
    ppermute x1 -> x6, local copies, waits for them, and re-layouts: 1.28 us -> 10.5 us  [_gather_blocks(): got = lax.ppermute(x, axis, _xor_pairs(n, j))]
    dynamic_update_slice x0 -> x8, local copies, waits for them, and re-layouts: none -> 8.62 us  [the longest x6 6.45 us: _gather_blocks(): full = lax.dynamic_update_slice_in_dim(full, got, (index ^ j) * width, 1)]
    ppermute x1, starting transfers between devices: 9.86 us -> 2.47 us  [per_device(): block = lax.ppermute(block, ('traj', 'mstate'), col_pairs)]
  transfers between devices with their start and end apart: 47 -> 52, of which waited for: 31 -> 34; matrix products, arithmetic and copies ran while one was open for 20% -> 6% of each run, Pallas kernels for 0% -> 0%
where the time goes in v2:
time: 517 us; the launch traced here: 507 us
  other arithmetic  172 us (33%)
  waiting for transfers between devices  138 us (27%)
  local copies, waits for them, and re-layouts  108 us (21%)
  starting transfers between devices  88.1 us (17%)
    ppermute x36, waiting for transfers between devices, _tree(): lax.ppermute(x, axis, _xor_pairs(n, j * shift))  120 us
    scatter-add x2, other arithmetic, _frame_part(): local_total = jax.ops.segment_sum(weights.T, labels, num_segments=width).T  89.6 us
    ppermute x36, starting transfers between devices, _tree(): lax.ppermute(x, axis, _xor_pairs(n, j * shift))  65.2 us
    gather x2, local copies, waits for them, and re-layouts, _frame_part(): scores = jnp.take(level, labels, axis=1) - bias  58.5 us
    scatter-add x1, other arithmetic, per_device(): local_visits = jax.ops.segment_sum(states, labels, num_segments=width).T  44 us
    reduce_max x2, other arithmetic, _frame_part(): top = jnp.max(scores, axis=0)  13.1 us
    ppermute x9, starting transfers between devices, _scatter_blocks(): lax.ppermute(block(index ^ j), axis, _xor_pairs(n, j))  12.6 us
    ppermute x9, waiting for transfers between devices, _scatter_blocks(): lax.ppermute(block(index ^ j), axis, _xor_pairs(n, j))  12.2 us
  transfers between devices with their start and end apart: 52, of which 34 were waited for; matrix products, arithmetic and copies ran while one was open for 6% of the time, Pallas kernels for 0%

profile of v2, /device:TPU:1, one launch (start us, length us, event | category | flops | bytes accessed | tf_op | source)
XLA Modules:
  0.0 506.8 jit_solution(14503341488943496448)
XLA Ops:
  0.7 44.0 %scatter_custom_fusion = f32[4096,32]{1,0:T(8,128)S(1)} fusion(s32[8192]{0:T(1024)} %param.9, s32[8192]{0:T(1024)} %param.10, f32[]{:T(128)} %constant.23.clone.1), kind=kCustom, calls=%fused_computation.11 | custom fusion | flops 786432 | bytes 557568 | tf_op jit(solution)/shard_map/scatter-add | solution.py:105
  55.0 6.0 %multiply_reduce_fusion.1 = f32[32,1024]{1,0:T(8,128)S(1)} fusion(s32[32,64,1024]{2,1,0:T(8,128)} %param.11, f32[32,1024]{1,0:T(8,128)S(1)} %get-tuple-element.101, f32[32,64]{1,0:T(8,128)S(1)} %get-tuple-element.103, f32[32,64]{1,0:T(8,128)S(1)} %get-tuple-element.104, f32[32,1024]{1,0:T(8,128)S(1)} %get-tuple-element.102), kind=kLoop, calls=%fused_computation.6 | loop fusion | flops 18841600 | bytes 8798208 | tf_op jit(solution)/shard_map/reduce_sum | solution.py:80
  66.4 6.0 %collective-permute-done.4 = f32[32,2048]{1,0:T(8,128)S(1)} collective-permute-done((f32[32,2048]{1,0:T(8,128)S(1)}, f32[32,2048]{1,0:T(8,128)S(1)}, u32[]{:S(2)}, u32[]{:S(2)}) %collective-permute-start.4) | collective-permute-done | bytes 262176 | tf_op jit(solution)/shard_map/ppermute | solution.py:27
  72.5 5.9 %collective-permute-done.5 = f32[32,2048]{1,0:T(8,128)S(1)} collective-permute-done((f32[32,2048]{1,0:T(8,128)S(1)}, f32[32,2048]{1,0:T(8,128)S(1)}, u32[]{:S(2)}, u32[]{:S(2)}) %collective-permute-start.5) | collective-permute-done | bytes 262176 | tf_op jit(solution)/shard_map/ppermute | solution.py:27
  82.6 5.1 %collective-permute-done.6 = f32[32,2048]{1,0:T(8,128)S(1)} collective-permute-done((f32[32,2048]{1,0:T(8,128)S(1)}, f32[32,2048]{1,0:T(8,128)S(1)}, u32[]{:S(2)}, u32[]{:S(2)}) %collective-permute-start.6) | collective-permute-done | bytes 262176 | tf_op jit(solution)/shard_map/ppermute | solution.py:27
  87.7 6.5 %collective-permute-done.8 = f32[32,2048]{1,0:T(8,128)S(1)} collective-permute-done((f32[32,2048]{1,0:T(8,128)S(1)}, f32[32,2048]{1,0:T(8,128)S(1)}, u32[]{:S(2)}, u32[]{:S(2)}) %collective-permute-start.8) | collective-permute-done | bytes 262176 | tf_op jit(solution)/shard_map/ppermute | solution.py:27
  94.3 5.4 %collective-permute-start.10 = (f32[32,2048]{1,0:T(8,128)S(1)}, f32[32,2048]{1,0:T(8,128)S(1)}, u32[]{:S(2)}, u32[]{:S(2)}) collective-permute-start(f32[32,2048]{1,0:T(8,128)S(1)} %add_add_fusion.1), channel_id=1, source_target_pairs={{0,128},{4,132},{8,136},{12,140},{16,144},{20,148},{24,152},{28,15... | collective-permute-start | bytes 786440 | tf_op jit(solution)/shard_map/ppermute | solution.py:27
  101.7 4.8 collective-permute-done.10
  106.5 15.5 %collective-permute-done.11 = f32[32,2048]{1,0:T(8,128)S(1)} collective-permute-done((f32[32,2048]{1,0:T(8,128)S(1)}, f32[32,2048]{1,0:T(8,128)S(1)}, u32[]{:S(2)}, u32[]{:S(2)}) %collective-permute-start.11) | collective-permute-done | bytes 262176 | tf_op jit(solution)/shard_map/ppermute | solution.py:27
  143.3 30.6 %gather_fusion = f32[8192,32]{1,0:T(8,128)} fusion(f32[32,4096]{0,1:T(8,128)S(1)} %constant_dynamic-update-slice_fusion.4, s32[8192]{0:T(1024)} %fusion.59), kind=kCustom, calls=%fused_computation.clone | custom fusion | bytes 2129920 | tf_op jit(solution)/shard_map/jit(_take)/gather | solution.py:63
  173.9 6.5 %fusion.8 = f32[8192]{0:T(1024)S(1)} fusion(f32[32,8192]{0,1:T(8,128)} %copy.318, f32[8192,32]{1,0:T(8,128)} %gather_fusion, pred[8192]{0:T(1024)(128)(4,1)S(1)} %compare_and_fusion), kind=kLoop, calls=%fused_computation.24 | loop fusion | flops 778240 | bytes 2138112 | tf_op jit(solution)/shard_map/reduce_max | solution.py:64
  187.7 44.8 %scatter_custom_fusion.1 = f32[4096,32]{1,0:T(8,128)S(1)} fusion(s32[8192]{0:T(1024)} %param.9, f32[8192,32]{1,0:T(8,128)} %copy.319, f32[]{:T(128)} %constant.23.clone.1), kind=kCustom, calls=%fused_computation.19 | custom fusion | flops 262144 | bytes 524800 | tf_op jit(solution)/shard_map/scatter-add | solution.py:69
  278.3 9.7 %collective-permute-done.24 = f32[32,1025]{1,0:T(8,128)S(1)} collective-permute-done((f32[32,1025]{1,0:T(8,128)S(1)}, f32[32,1025]{1,0:T(8,128)S(1)}, u32[]{:S(2)}, u32[]{:S(2)}) %collective-permute-start.24) | collective-permute-done | bytes 131232 | tf_op jit(solution)/shard_map/ppermute | solution.py:27
  292.7 5.1 %collective-permute-done.27 = f32[2,32,64]{2,1,0:T(8,128)S(1)} collective-permute-done((f32[2,32,64]{2,1,0:T(8,128)S(1)}, f32[2,32,64]{2,1,0:T(8,128)S(1)}, u32[]{:S(2)}, u32[]{:S(2)}) %collective-permute-start.27) | collective-permute-done | bytes 16416 | tf_op jit(solution)/shard_map/ppermute | solution.py:133
  297.8 6.0 %multiply_reduce_fusion = f32[32,1024]{1,0:T(8,128)S(1)} fusion(s32[32,64,1024]{2,1,0:T(8,128)} %param.11, f32[32,1024]{1,0:T(8,128)S(1)} %fusion.38, f32[32,64]{1,0:T(8,128)S(1)} %get-tuple-element.58, f32[32,64]{1,0:T(8,128)S(1)} %get-tuple-element.57, f32[32,1024]{1,0:T(8,128)S(1)} %get-tuple-element.55), kind=kLoop, calls=%fused_computation.5 | loop fusion | flops 18841600 | bytes 8798208 | tf_op jit(solution)/shard_map/reduce_sum | solution.py:80
  313.1 4.8 collective-permute-start.31
  330.4 5.4 %collective-permute-start.35 = (f32[32,1024]{1,0:T(8,128)S(1)}, f32[32,1024]{1,0:T(8,128)S(1)}, u32[]{:S(2)}, u32[]{:S(2)}) collective-permute-start(f32[32,1024]{1,0:T(8,128)S(1)} %add_add_fusion.3), channel_id=1, source_target_pairs={{0,128},{4,132},{8,136},{12,140},{16,144},{20,148},{24,152},{28,15... | collective-permute-start | bytes 393224 | tf_op jit(solution)/shard_map/ppermute | solution.py:27
  335.8 6.9 %collective-permute-done.34 = f32[32,1024]{1,0:T(8,128)S(1)} collective-permute-done((f32[32,1024]{1,0:T(8,128)S(1)}, f32[32,1024]{1,0:T(8,128)S(1)}, u32[]{:S(2)}, u32[]{:S(2)}) %collective-permute-start.34) | collective-permute-done | bytes 131104 | tf_op jit(solution)/shard_map/ppermute | solution.py:27
  361.9 27.9 %gather_fusion.1 = f32[8192,32]{1,0:T(8,128)} fusion(f32[32,4096]{0,1:T(8,128)S(1)} %constant_dynamic-update-slice_fusion, s32[8192]{0:T(1024)S(1)} %copy-done.5), kind=kCustom, calls=%fused_computation.1.clone | custom fusion | bytes 2129920 | tf_op jit(solution)/shard_map/jit(_take)/gather | solution.py:63
  389.8 6.5 %fusion.9 = f32[8192]{0:T(1024)S(1)} fusion(f32[32,8192]{0,1:T(8,128)} %copy.318, f32[8192,32]{1,0:T(8,128)} %gather_fusion.1, pred[8192]{0:T(1024)(128)(4,1)S(1)} %compare_and_fusion), kind=kLoop, calls=%fused_computation.25 | loop fusion | flops 778240 | bytes 2138112 | tf_op jit(solution)/shard_map/reduce_max | solution.py:64
  403.5 44.8 %scatter_custom_fusion.2 = f32[4096,32]{1,0:T(8,128)S(1)} fusion(s32[8192]{0:T(1024)} %param.9, f32[8192,32]{1,0:T(8,128)} %copy.347, f32[]{:T(128)} %constant.23.clone.1), kind=kCustom, calls=%fused_computation.17 | custom fusion | flops 262144 | bytes 524800 | tf_op jit(solution)/shard_map/scatter-add | solution.py:69
  473.3 4.4 collective-permute-start.46
  488.0 4.8 collective-permute-start.50
  492.7 8.3 %collective-permute-done.49 = f32[32,1025]{1,0:T(8,128)S(1)} collective-permute-done((f32[32,1025]{1,0:T(8,128)S(1)}, f32[32,1025]{1,0:T(8,128)S(1)}, u32[]{:S(2)}, u32[]{:S(2)}) %collective-permute-start.49) | collective-permute-done | bytes 131232 | tf_op jit(solution)/shard_map/ppermute | solution.py:27
  (256 shorter events, 189.5 us)
Async XLA Ops:
  47.0 14.1 %collective-permute-start = (f32[32,1024]{1,0:T(8,128)S(1)}, f32[32,1024]{1,0:T(8,128)S(1)}, u32[]{:S(2)}, u32[]{:S(2)}) collective-permute-start(f32[32,1024]{1,0:T(8,128)S(1)} %bitcast.173), channel_id=1, source_target_pairs={{0,1},{1,0},{2,3},{3,2},{4,5},{5,4},{6,7},{7,6},{8,9},{9,8},{10,11... | collective-permute-start | bytes 393224 | tf_op jit(solution)/shard_map/ppermute | solution.py:45
  50.4 10.8 %collective-permute-start.1 = (f32[32,1024]{1,0:T(8,128)S(1)}, f32[32,1024]{1,0:T(8,128)S(1)}, u32[]{:S(2)}, u32[]{:S(2)}) collective-permute-start(f32[32,1024]{1,0:T(8,128)S(1)} %bitcast.174), channel_id=1, source_target_pairs={{0,2},{1,3},{2,0},{3,1},{4,6},{5,7},{6,4},{7,5},{8,10},{9,11},{10,... | collective-permute-start | bytes 393224 | tf_op jit(solution)/shard_map/ppermute | solution.py:45
  64.7 13.6 %collective-permute-start.5 = (f32[32,2048]{1,0:T(8,128)S(1)}, f32[32,2048]{1,0:T(8,128)S(1)}, u32[]{:S(2)}, u32[]{:S(2)}) collective-permute-start(f32[32,2048]{1,0:T(8,128)S(1)} %pad_maximum_fusion), channel_id=1, source_target_pairs={{0,12},{4,8},{8,4},{12,0},{16,28},{20,24},{24,20},{28,16},{32,44},... | collective-permute-start | bytes 786440 | tf_op jit(solution)/shard_map/ppermute | solution.py:27
  78.4 9.3 %collective-permute-start.6 = (f32[32,2048]{1,0:T(8,128)S(1)}, f32[32,2048]{1,0:T(8,128)S(1)}, u32[]{:S(2)}, u32[]{:S(2)}) collective-permute-start(f32[32,2048]{1,0:T(8,128)S(1)} %add_add_fusion.2), channel_id=1, source_target_pairs={{0,16},{4,20},{8,24},{12,28},{16,0},{20,4},{24,8},{28,12},{32,48},... | collective-permute-start | bytes 786440 | tf_op jit(solution)/shard_map/ppermute | solution.py:27
  81.3 12.9 %collective-permute-start.8 = (f32[32,2048]{1,0:T(8,128)S(1)}, f32[32,2048]{1,0:T(8,128)S(1)}, u32[]{:S(2)}, u32[]{:S(2)}) collective-permute-start(f32[32,2048]{1,0:T(8,128)S(1)} %add_add_fusion.2), channel_id=1, source_target_pairs={{0,48},{4,52},{8,56},{12,60},{16,32},{20,36},{24,40},{28,44},{32,1... | collective-permute-start | bytes 786440 | tf_op jit(solution)/shard_map/ppermute | solution.py:27
  94.3 12.2 %collective-permute-start.10 = (f32[32,2048]{1,0:T(8,128)S(1)}, f32[32,2048]{1,0:T(8,128)S(1)}, u32[]{:S(2)}, u32[]{:S(2)}) collective-permute-start(f32[32,2048]{1,0:T(8,128)S(1)} %add_add_fusion.1), channel_id=1, source_target_pairs={{0,128},{4,132},{8,136},{12,140},{16,144},{20,148},{24,152},{28,15... | collective-permute-start | bytes 786440 | tf_op jit(solution)/shard_map/ppermute | solution.py:27
  99.7 22.3 %collective-permute-start.11 = (f32[32,2048]{1,0:T(8,128)S(1)}, f32[32,2048]{1,0:T(8,128)S(1)}, u32[]{:S(2)}, u32[]{:S(2)}) collective-permute-start(f32[32,2048]{1,0:T(8,128)S(1)} %add_add_fusion.1), channel_id=1, source_target_pairs={{0,192},{4,196},{8,200},{12,204},{16,208},{20,212},{24,216},{28,22... | collective-permute-start | bytes 786440 | tf_op jit(solution)/shard_map/ppermute | solution.py:27
  99.7 24.1 %collective-permute-start.9 = (f32[32,2048]{1,0:T(8,128)S(1)}, f32[32,2048]{1,0:T(8,128)S(1)}, u32[]{:S(2)}, u32[]{:S(2)}) collective-permute-start(f32[32,2048]{1,0:T(8,128)S(1)} %add_add_fusion.1), channel_id=1, source_target_pairs={{0,64},{4,68},{8,72},{12,76},{16,80},{20,84},{24,88},{28,92},{32,9... | collective-permute-start | bytes 786440 | tf_op jit(solution)/shard_map/ppermute | solution.py:27
  124.6 9.7 %collective-permute-start.12 = (f32[32,1024]{1,0:T(8,128)}, f32[32,1024]{1,0:T(8,128)}, u32[]{:S(2)}, u32[]{:S(2)}) collective-permute-start(f32[32,1024]{1,0:T(8,128)} %get-tuple-element.56), channel_id=1, source_target_pairs={{0,1},{1,0},{2,3},{3,2},{4,5},{5,4},{6,7},{7,6},{8,9},{9,8},{10,11... | collective-permute-start | bytes 393224 | tf_op jit(solution)/shard_map/ppermute | solution.py:57
  238.2 8.6 %collective-permute-start.16 = (f32[32,1025]{1,0:T(8,128)S(1)}, f32[32,1025]{1,0:T(8,128)S(1)}, u32[]{:S(2)}, u32[]{:S(2)}) collective-permute-start(f32[32,1025]{1,0:T(8,128)S(1)} %get-tuple-element.63), channel_id=1, source_target_pairs={{0,2},{1,3},{2,0},{3,1},{4,6},{5,7},{6,4},{7,5},{8,10},{9,11},{10,... | collective-permute-start | bytes 393608 | tf_op jit(solution)/shard_map/ppermute | solution.py:45
  241.4 8.3 %collective-permute-start.17 = (f32[32,1025]{1,0:T(8,128)S(1)}, f32[32,1025]{1,0:T(8,128)S(1)}, u32[]{:S(2)}, u32[]{:S(2)}) collective-permute-start(f32[32,1025]{1,0:T(8,128)S(1)} %get-tuple-element.62), channel_id=1, source_target_pairs={{0,3},{1,2},{2,1},{3,0},{4,7},{5,6},{6,5},{7,4},{8,11},{9,10},{10,... | collective-permute-start | bytes 393608 | tf_op jit(solution)/shard_map/ppermute | solution.py:45
  272.4 15.6 %collective-permute-start.24 = (f32[32,1025]{1,0:T(8,128)S(1)}, f32[32,1025]{1,0:T(8,128)S(1)}, u32[]{:S(2)}, u32[]{:S(2)}) collective-permute-start(f32[32,1025]{1,0:T(8,128)S(1)} %pad_maximum_fusion.9), channel_id=1, source_target_pairs={{0,64},{4,68},{8,72},{12,76},{16,80},{20,84},{24,88},{28,92},{32,9... | collective-permute-start | bytes 393608 | tf_op jit(solution)/shard_map/ppermute | solution.py:27
  274.2 13.9 %collective-permute-start.25 = (f32[32,1025]{1,0:T(8,128)S(1)}, f32[32,1025]{1,0:T(8,128)S(1)}, u32[]{:S(2)}, u32[]{:S(2)}) collective-permute-start(f32[32,1025]{1,0:T(8,128)S(1)} %pad_maximum_fusion.9), channel_id=1, source_target_pairs={{0,128},{4,132},{8,136},{12,140},{16,144},{20,148},{24,152},{28,15... | collective-permute-start | bytes 393608 | tf_op jit(solution)/shard_map/ppermute | solution.py:27
  277.2 12.7 %collective-permute-start.26 = (f32[32,1025]{1,0:T(8,128)S(1)}, f32[32,1025]{1,0:T(8,128)S(1)}, u32[]{:S(2)}, u32[]{:S(2)}) collective-permute-start(f32[32,1025]{1,0:T(8,128)S(1)} %pad_maximum_fusion.9), channel_id=1, source_target_pairs={{0,192},{4,196},{8,200},{12,204},{16,208},{20,212},{24,216},{28,22... | collective-permute-start | bytes 393608 | tf_op jit(solution)/shard_map/ppermute | solution.py:27
  313.1 9.2 %collective-permute-start.31 = (f32[32,1024]{1,0:T(8,128)S(1)}, f32[32,1024]{1,0:T(8,128)S(1)}, u32[]{:S(2)}, u32[]{:S(2)}) collective-permute-start(f32[32,1024]{1,0:T(8,128)S(1)} %add_add_fusion.4), channel_id=1, source_target_pairs={{0,16},{4,20},{8,24},{12,28},{16,0},{20,4},{24,8},{28,12},{32,48},... | collective-permute-start | bytes 393224 | tf_op jit(solution)/shard_map/ppermute | solution.py:27
  329.1 13.7 %collective-permute-start.34 = (f32[32,1024]{1,0:T(8,128)S(1)}, f32[32,1024]{1,0:T(8,128)S(1)}, u32[]{:S(2)}, u32[]{:S(2)}) collective-permute-start(f32[32,1024]{1,0:T(8,128)S(1)} %add_add_fusion.3), channel_id=1, source_target_pairs={{0,64},{4,68},{8,72},{12,76},{16,80},{20,84},{24,88},{28,92},{32,9... | collective-permute-start | bytes 393224 | tf_op jit(solution)/shard_map/ppermute | solution.py:27
  330.4 14.1 %collective-permute-start.35 = (f32[32,1024]{1,0:T(8,128)S(1)}, f32[32,1024]{1,0:T(8,128)S(1)}, u32[]{:S(2)}, u32[]{:S(2)}) collective-permute-start(f32[32,1024]{1,0:T(8,128)S(1)} %add_add_fusion.3), channel_id=1, source_target_pairs={{0,128},{4,132},{8,136},{12,140},{16,144},{20,148},{24,152},{28,15... | collective-permute-start | bytes 393224 | tf_op jit(solution)/shard_map/ppermute | solution.py:27
  335.8 11.1 %collective-permute-start.36 = (f32[32,1024]{1,0:T(8,128)S(1)}, f32[32,1024]{1,0:T(8,128)S(1)}, u32[]{:S(2)}, u32[]{:S(2)}) collective-permute-start(f32[32,1024]{1,0:T(8,128)S(1)} %add_add_fusion.3), channel_id=1, source_target_pairs={{0,192},{4,196},{8,200},{12,204},{16,208},{20,212},{24,216},{28,22... | collective-permute-start | bytes 393224 | tf_op jit(solution)/shard_map/ppermute | solution.py:27
  348.6 11.2 %collective-permute-start.39 = (f32[32,1024]{1,0:T(8,128)S(1)}, f32[32,1024]{1,0:T(8,128)S(1)}, u32[]{:S(2)}, u32[]{:S(2)}) collective-permute-start(f32[32,1024]{1,0:T(8,128)S(1)} %get-tuple-element.27), channel_id=1, source_target_pairs={{0,3},{1,2},{2,1},{3,0},{4,7},{5,6},{6,5},{7,4},{8,11},{9,10},{10,... | collective-permute-start | bytes 393224 | tf_op jit(solution)/shard_map/ppermute | solution.py:57
  464.2 8.7 %collective-permute-start.45 = (f32[32,1025]{1,0:T(8,128)S(1)}, f32[32,1025]{1,0:T(8,128)S(1)}, u32[]{:S(2)}, u32[]{:S(2)}) collective-permute-start(f32[32,1025]{1,0:T(8,128)S(1)} %pad_maximum_fusion.10), channel_id=1, source_target_pairs={{0,12},{4,8},{8,4},{12,0},{16,28},{20,24},{24,20},{28,16},{32,44},... | collective-permute-start | bytes 393608 | tf_op jit(solution)/shard_map/ppermute | solution.py:27
  473.3 8.5 %collective-permute-start.46 = (f32[32,1025]{1,0:T(8,128)S(1)}, f32[32,1025]{1,0:T(8,128)S(1)}, u32[]{:S(2)}, u32[]{:S(2)}) collective-permute-start(f32[32,1025]{1,0:T(8,128)S(1)} %pad_maximum_fusion.11), channel_id=1, source_target_pairs={{0,16},{4,20},{8,24},{12,28},{16,0},{20,4},{24,8},{28,12},{32,48},... | collective-permute-start | bytes 393608 | tf_op jit(solution)/shard_map/ppermute | solution.py:27
  485.7 15.3 %collective-permute-start.49 = (f32[32,1025]{1,0:T(8,128)S(1)}, f32[32,1025]{1,0:T(8,128)S(1)}, u32[]{:S(2)}, u32[]{:S(2)}) collective-permute-start(f32[32,1025]{1,0:T(8,128)S(1)} %pad_maximum_fusion.12), channel_id=1, source_target_pairs={{0,64},{4,68},{8,72},{12,76},{16,80},{20,84},{24,88},{28,92},{32,9... | collective-permute-start | bytes 393608 | tf_op jit(solution)/shard_map/ppermute | solution.py:27
  488.0 16.4 %collective-permute-start.50 = (f32[32,1025]{1,0:T(8,128)S(1)}, f32[32,1025]{1,0:T(8,128)S(1)}, u32[]{:S(2)}, u32[]{:S(2)}) collective-permute-start(f32[32,1025]{1,0:T(8,128)S(1)} %pad_maximum_fusion.12), channel_id=1, source_target_pairs={{0,128},{4,132},{8,136},{12,140},{16,144},{20,148},{24,152},{28,15... | collective-permute-start | bytes 393608 | tf_op jit(solution)/shard_map/ppermute | solution.py:27
  492.7 13.0 %collective-permute-start.51 = (f32[32,1025]{1,0:T(8,128)S(1)}, f32[32,1025]{1,0:T(8,128)S(1)}, u32[]{:S(2)}, u32[]{:S(2)}) collective-permute-start(f32[32,1025]{1,0:T(8,128)S(1)} %pad_maximum_fusion.12), channel_id=1, source_target_pairs={{0,192},{4,196},{8,200},{12,204},{16,208},{20,212},{24,216},{28,22... | collective-permute-start | bytes 393608 | tf_op jit(solution)/shard_map/ppermute | solution.py:27
  (35 other events, 321.8 us)

commit v3 on v2

--- a/solution.py
+++ b/solution.py
@@ -1,6 +1,8 @@
 import jax
 import jax.numpy as jnp
 from jax import lax
+from jax.experimental import pallas as pl
+from jax.experimental.pallas import tpu as pltpu
 from jax.sharding import PartitionSpec as P
 
 ITERS = 2
@@ -59,14 +61,66 @@
     return full
 
 
-def _frame_part(level, bias, labels, width):
-    scores = jnp.take(level, labels, axis=1) - bias
-    top = jnp.max(scores, axis=0)
-    logl = top + jnp.log(jnp.sum(jnp.exp(scores - top[None, :]), axis=0))
-    term = -bias - logl[None, :]
-    local_top = jnp.max(term, axis=1)
-    weights = jnp.exp(term - local_top[:, None])
-    local_total = jax.ops.segment_sum(weights.T, labels, num_segments=width).T
+def _scatter_kernel(lab_ref, w_ref, o_ref, *accs):
+    unroll = len(accs)
+    for acc in accs:
+        acc[...] = jnp.zeros_like(acc)
+
+    def body(c, carry):
+        base = c * unroll
+        for j in range(unroll):
+            x = base + j
+            i = lab_ref[x]
+            accs[j][pl.ds(i, 1), :] += w_ref[pl.ds(x, 1), :]
+        return carry
+
+    lax.fori_loop(0, w_ref.shape[0] // unroll, body, 0)
+    total = accs[0][...]
+    for acc in accs[1:]:
+        total = total + acc[...]
+    o_ref[...] = total
+
+
+def _seg_rows(w_t, labels, width, unroll=8):
+    return pl.pallas_call(
+        _scatter_kernel,
+        in_specs=[pl.BlockSpec(memory_space=pltpu.SMEM), pl.BlockSpec(memory_space=pltpu.VMEM)],
+        out_specs=pl.BlockSpec(memory_space=pltpu.VMEM),
+        out_shape=jax.ShapeDtypeStruct((width, w_t.shape[1]), jnp.float32),
+        scratch_shapes=[pltpu.VMEM((width, w_t.shape[1]), jnp.float32)] * unroll,
+    )(labels, w_t)
+
+
+def _gather_kernel(lab_ref, lev_ref, o_ref):
+    unroll = 16
+
+    def body(c, carry):
+        base = c * unroll
+        for j in range(unroll):
+            x = base + j
+            o_ref[pl.ds(x, 1), :] = lev_ref[pl.ds(lab_ref[x], 1), :]
+        return carry
+
+    lax.fori_loop(0, o_ref.shape[0] // unroll, body, 0)
+
+
+def _take_rows(lev_t, labels):
+    return pl.pallas_call(
+        _gather_kernel,
+        in_specs=[pl.BlockSpec(memory_space=pltpu.SMEM), pl.BlockSpec(memory_space=pltpu.VMEM)],
+        out_specs=pl.BlockSpec(memory_space=pltpu.VMEM),
+        out_shape=jax.ShapeDtypeStruct((labels.shape[0], lev_t.shape[1]), lev_t.dtype),
+    )(labels, lev_t)
+
+
+def _frame_part(level, bias_t, labels, width):
+    scores = _take_rows(level.T, labels) - bias_t
+    top = jnp.max(scores, axis=1)
+    logl = top + jnp.log(jnp.sum(jnp.exp(scores - top[:, None]), axis=1))
+    term = -bias_t - logl[:, None]
+    local_top = jnp.max(term, axis=0)
+    weights = jnp.exp(term - local_top[None, :])
+    local_total = _seg_rows(weights, labels, width).T
     return local_top, local_total
 
 
@@ -102,7 +156,8 @@
     col_offset = (traj_at // n_mstate) * col_count
 
     states = jax.nn.one_hot(therm_index, states_k, dtype=jnp.float32)
-    local_visits = jax.ops.segment_sum(states, labels, num_segments=width).T
+    local_visits = _seg_rows(states, labels, width).T
+    bias_t = bias.T
     visits_part = _scatter_blocks(local_visits, "mstate", n_mstate, _add)
     counts_real = counts.astype(jnp.float32)
 
@@ -121,7 +176,7 @@
         mult_rows = jnp.log(0.5 + row_total)
         level_rows = jnp.log(jnp.exp(mult_rows) + visits_rows) + free_rows
         level = _gather_blocks(level_rows, "mstate", n_mstate)
-        local_top, local_total = _frame_part(level, bias, labels, width)
+        local_top, local_total = _frame_part(level, bias_t, labels, width)
         packed = _scatter_blocks(local_total, "mstate", n_mstate, _lse_merge, local_top[:, None])
         packed = _tree(packed, "traj", n_traj, _lse_merge)
         free_rows = -(packed[:, -1:] + jnp.log(packed[:, :-1]))

time: 517 us -> 561 us (1.085)
  waiting for transfers between devices: 138 us -> 251 us
  other arithmetic: 172 us -> 66 us
  Pallas kernels: 0 us -> 76.6 us
  local copies, waits for them, and re-layouts: 108 us -> 44.7 us
  starting transfers between devices: 88.1 us -> 111 us
    scatter-add x3 -> x0, other arithmetic: 134 us -> none  [the longest x2 89.6 us: _frame_part(): local_total = jax.ops.segment_sum(weights.T, labels, num_segments=width).T]
    pallas_call x0 -> x5, Pallas kernels: none -> 76.6 us  [the longest x3 51.6 us: _seg_rows(): pl.pallas_call(_scatter_kernel, in_specs=[pl.BlockSpec(memory_space=pltpu...]
    ppermute x36, waiting for transfers between devices: 120 us -> 179 us  [_tree(): lax.ppermute(x, axis, _xor_pairs(n, j * shift))]
    gather x2 -> x0, local copies, waits for them, and re-layouts: 58.5 us -> none  [_frame_part(): scores = jnp.take(level, labels, axis=1) - bias]
    ppermute x6, waiting for transfers between devices: 0.02 us -> 40.6 us  [_gather_blocks(): got = lax.ppermute(x, axis, _xor_pairs(n, j))]
    ppermute x9, waiting for transfers between devices: 12.2 us -> 27.2 us  [_scatter_blocks(): lax.ppermute(block(index ^ j), axis, _xor_pairs(n, j))]
    unnamed x45 -> x72, local copies, waits for them, and re-layouts: 8.75 us -> 22 us
    ppermute x9, starting transfers between devices: 12.6 us -> 25.3 us  [_scatter_blocks(): lax.ppermute(block(index ^ j), axis, _xor_pairs(n, j))]
  transfers between devices with their start and end apart: 52 -> 52, of which waited for: 34 -> 43; matrix products, arithmetic and copies ran while one was open for 6% -> 4% of each run, Pallas kernels for 0% -> 0%
where the time goes in v3:
time: 561 us; the launch traced here: 552 us
  waiting for transfers between devices  251 us (45%)
  starting transfers between devices  111 us (20%)
  Pallas kernels  76.6 us (14%)
  other arithmetic  66 us (12%)
  local copies, waits for them, and re-layouts  44.7 us (8%)
    ppermute x36, waiting for transfers between devices, _tree(): lax.ppermute(x, axis, _xor_pairs(n, j * shift))  179 us
    ppermute x36, starting transfers between devices, _tree(): lax.ppermute(x, axis, _xor_pairs(n, j * shift))  75.6 us
    pallas_call x3, Pallas kernels, _seg_rows(): pl.pallas_call(_scatter_kernel, in_specs=[pl.BlockSpec(memory_space=pltpu...  51.6 us
    ppermute x6, waiting for transfers between devices, _gather_blocks(): got = lax.ppermute(x, axis, _xor_pairs(n, j))  40.6 us
    ppermute x9, waiting for transfers between devices, _scatter_blocks(): lax.ppermute(block(index ^ j), axis, _xor_pairs(n, j))  27.2 us
    ppermute x9, starting transfers between devices, _scatter_blocks(): lax.ppermute(block(index ^ j), axis, _xor_pairs(n, j))  25.3 us
    pallas_call x2, Pallas kernels, _take_rows(): pl.pallas_call(_gather_kernel, in_specs=[pl.BlockSpec(memory_space=pltpu....  25 us
    unnamed x72, local copies, waits for them, and re-layouts  22 us
  transfers between devices with their start and end apart: 52, of which 43 were waited for; matrix products, arithmetic and copies ran while one was open for 4% of the time, Pallas kernels for 0%

profile of v3, /device:TPU:1, one launch (start us, length us, event | category | flops | bytes accessed | tf_op | source)
XLA Modules:
  0.0 551.7 jit_solution(9278093629096071720)
XLA Ops:
  6.2 17.2 %shard_map.77 = f32[4096,32]{1,0:T(8,128)} custom-call(s32[8192]{0:T(1024)} %lab_ref.9, f32[8192,32]{1,0:T(8,128)} %fusion.w_ref), custom_call_target="tpu_custom_call" | custom-call | tf_op jit(solution)/shard_map/pallas_call | solution.py:85
  31.3 6.0 %multiply_reduce_fusion.1 = f32[32,1024]{1,0:T(8,128)S(1)} fusion(s32[32,64,1024]{2,1,0:T(8,128)} %param.9, f32[32,1024]{1,0:T(8,128)S(1)} %get-tuple-element.101, f32[32,64]{1,0:T(8,128)S(1)} %get-tuple-element.103, f32[32,64]{1,0:T(8,128)S(1)} %get-tuple-element.104, f32[32,1024]{1,0:T(8,128)S(1)} %get-tuple-element.102), kind=kLoop, calls=%fused_computation.1 | loop fusion | flops 18841600 | bytes 8798208 | tf_op jit(solution)/shard_map/reduce_sum | solution.py:134
  37.6 14.6 %collective-permute-done.1 = f32[32,1024]{0,1:T(8,128)} collective-permute-done((f32[32,1024]{0,1:T(8,128)S(1)}, f32[32,1024]{0,1:T(8,128)}, u32[]{:S(2)}, u32[]{:S(2)}) %collective-permute-start.1) | collective-permute-done | bytes 131104 | tf_op jit(solution)/shard_map/ppermute | solution.py:47
  60.3 5.7 %collective-permute-done.4 = f32[32,2048]{1,0:T(8,128)S(1)} collective-permute-done((f32[32,2048]{1,0:T(8,128)S(1)}, f32[32,2048]{1,0:T(8,128)S(1)}, u32[]{:S(2)}, u32[]{:S(2)}) %collective-permute-start.4) | collective-permute-done | bytes 262176 | tf_op jit(solution)/shard_map/ppermute | solution.py:29
  104.1 16.8 %collective-permute-done.9 = f32[32,2048]{1,0:T(8,128)S(1)} collective-permute-done((f32[32,2048]{1,0:T(8,128)S(1)}, f32[32,2048]{1,0:T(8,128)S(1)}, u32[]{:S(2)}, u32[]{:S(2)}) %collective-permute-start.9) | collective-permute-done | bytes 262176 | tf_op jit(solution)/shard_map/ppermute | solution.py:29
  139.1 10.1 %collective-permute-done.13 = f32[32,1024]{0,1:T(8,128)} collective-permute-done((f32[32,1024]{0,1:T(8,128)}, f32[32,1024]{0,1:T(8,128)}, u32[]{:S(2)}, u32[]{:S(2)}) %collective-permute-start.13) | collective-permute-done | bytes 131104 | tf_op jit(solution)/shard_map/ppermute | solution.py:59
  150.3 6.7 %collective-permute-done.14 = f32[32,1024]{0,1:T(8,128)S(1)} collective-permute-done((f32[32,1024]{0,1:T(8,128)}, f32[32,1024]{0,1:T(8,128)S(1)}, u32[]{:S(2)}, u32[]{:S(2)}) %collective-permute-start.14) | collective-permute-done | bytes 131104 | tf_op jit(solution)/shard_map/ppermute | solution.py:59
  158.3 12.5 %shard_map.78 = f32[8192,32]{1,0:T(8,128)} custom-call(s32[8192]{0:T(1024)} %lab_ref.9, f32[4096,32]{1,0:T(8,128)} %bitcast.201), custom_call_target="tpu_custom_call" | custom-call | tf_op jit(solution)/shard_map/pallas_call | solution.py:108
  187.4 17.2 %shard_map.79 = f32[4096,32]{1,0:T(8,128)} custom-call(s32[8192]{0:T(1024)} %lab_ref.9, f32[8192,32]{1,0:T(8,128)} %subtract_exponential_fusion.1.w_ref), custom_call_target="tpu_custom_call" | custom-call | tf_op jit(solution)/shard_map/pallas_call | solution.py:85
  206.7 12.9 %collective-permute-start.15 = (f32[32,1025]{1,0:T(8,128)S(1)}, f32[32,1025]{1,0:T(8,128)S(1)}, u32[]{:S(2)}, u32[]{:S(2)}) collective-permute-start(f32[32,1025]{1,0:T(8,128)S(1)} %get-tuple-element.64), channel_id=1, source_target_pairs={{0,1},{1,0},{2,3},{3,2},{4,5},{5,4},{6,7},{7,6},{8,9},{9,8},{10,11... | collective-permute-start | bytes 393608 | tf_op jit(solution)/shard_map/ppermute | solution.py:47
  273.0 9.0 %collective-permute-done.24 = f32[32,1025]{1,0:T(8,128)S(1)} collective-permute-done((f32[32,1025]{1,0:T(8,128)S(1)}, f32[32,1025]{1,0:T(8,128)S(1)}, u32[]{:S(2)}, u32[]{:S(2)}) %collective-permute-start.24) | collective-permute-done | bytes 131232 | tf_op jit(solution)/shard_map/ppermute | solution.py:29
  296.2 6.0 %multiply_reduce_fusion = f32[32,1024]{1,0:T(8,128)S(1)} fusion(s32[32,64,1024]{2,1,0:T(8,128)} %param.9, f32[32,1024]{1,0:T(8,128)S(1)} %copy.298, f32[32,64]{1,0:T(8,128)S(1)} %get-tuple-element.58, f32[32,64]{1,0:T(8,128)S(1)} %get-tuple-element.57, f32[32,1024]{1,0:T(8,128)S(1)} %copy.259), kind=kLoop, calls=%fused_computation | loop fusion | flops 18841600 | bytes 8798208 | tf_op jit(solution)/shard_map/reduce_sum | solution.py:134
  304.6 11.3 %collective-permute-done.29 = f32[32,1024]{0,1:T(8,128)S(1)} collective-permute-done((f32[32,1024]{0,1:T(8,128)S(1)}, f32[32,1024]{0,1:T(8,128)S(1)}, u32[]{:S(2)}, u32[]{:S(2)}) %collective-permute-start.29) | collective-permute-done | bytes 131104 | tf_op jit(solution)/shard_map/ppermute | solution.py:29
  315.9 11.7 %collective-permute-done.30 = f32[32,1024]{0,1:T(8,128)S(1)} collective-permute-done((f32[32,1024]{0,1:T(8,128)S(1)}, f32[32,1024]{0,1:T(8,128)S(1)}, u32[]{:S(2)}, u32[]{:S(2)}) %collective-permute-start.30) | collective-permute-done | bytes 131104 | tf_op jit(solution)/shard_map/ppermute | solution.py:29
  327.7 5.7 %collective-permute-start.31 = (f32[32,1024]{0,1:T(8,128)S(1)}, f32[32,1024]{0,1:T(8,128)S(1)}, u32[]{:S(2)}, u32[]{:S(2)}) collective-permute-start(f32[32,1024]{0,1:T(8,128)S(1)} %add_add_fusion.4), channel_id=1, source_target_pairs={{0,16},{4,20},{8,24},{12,28},{16,0},{20,4},{24,8},{28,12},{32,48},... | collective-permute-start | bytes 393224 | tf_op jit(solution)/shard_map/ppermute | solution.py:29
  337.5 8.0 %collective-permute-done.31 = f32[32,1024]{0,1:T(8,128)S(1)} collective-permute-done((f32[32,1024]{0,1:T(8,128)S(1)}, f32[32,1024]{0,1:T(8,128)S(1)}, u32[]{:S(2)}, u32[]{:S(2)}) %collective-permute-start.31) | collective-permute-done | bytes 131104 | tf_op jit(solution)/shard_map/ppermute | solution.py:29
  349.4 11.3 %collective-permute-done.33 = f32[32,1024]{0,1:T(8,128)S(1)} collective-permute-done((f32[32,1024]{0,1:T(8,128)S(1)}, f32[32,1024]{0,1:T(8,128)S(1)}, u32[]{:S(2)}, u32[]{:S(2)}) %collective-permute-start.33) | collective-permute-done | bytes 131104 | tf_op jit(solution)/shard_map/ppermute | solution.py:29
  362.4 6.6 %collective-permute-start.35 = (f32[32,1024]{0,1:T(8,128)S(1)}, f32[32,1024]{0,1:T(8,128)S(1)}, u32[]{:S(2)}, u32[]{:S(2)}) collective-permute-start(f32[32,1024]{0,1:T(8,128)S(1)} %add_add_fusion.3), channel_id=1, source_target_pairs={{0,128},{4,132},{8,136},{12,140},{16,144},{20,148},{24,152},{28,15... | collective-permute-start | bytes 393224 | tf_op jit(solution)/shard_map/ppermute | solution.py:29
  369.0 39.5 %collective-permute-done.34 = f32[32,1024]{0,1:T(8,128)S(1)} collective-permute-done((f32[32,1024]{0,1:T(8,128)S(1)}, f32[32,1024]{0,1:T(8,128)S(1)}, u32[]{:S(2)}, u32[]{:S(2)}) %collective-permute-start.34) | collective-permute-done | bytes 131104 | tf_op jit(solution)/shard_map/ppermute | solution.py:29
  419.5 8.0 %collective-permute-done.37 = f32[32,1024]{0,1:T(8,128)S(1)} collective-permute-done((f32[32,1024]{0,1:T(8,128)S(1)}, f32[32,1024]{0,1:T(8,128)S(1)}, u32[]{:S(2)}, u32[]{:S(2)}) %collective-permute-start.37) | collective-permute-done | bytes 131104 | tf_op jit(solution)/shard_map/ppermute | solution.py:59
  427.5 9.3 %collective-permute-done.38 = f32[32,1024]{0,1:T(8,128)S(1)} collective-permute-done((f32[32,1024]{0,1:T(8,128)S(1)}, f32[32,1024]{0,1:T(8,128)S(1)}, u32[]{:S(2)}, u32[]{:S(2)}) %collective-permute-start.38) | collective-permute-done | bytes 131104 | tf_op jit(solution)/shard_map/ppermute | solution.py:59
  442.4 12.5 %shard_map.80 = f32[8192,32]{1,0:T(8,128)} custom-call(s32[8192]{0:T(1024)} %lab_ref.9, f32[4096,32]{1,0:T(8,128)} %bitcast.200), custom_call_target="tpu_custom_call" | custom-call | tf_op jit(solution)/shard_map/pallas_call | solution.py:108
  471.4 17.2 %shard_map.81 = f32[4096,32]{1,0:T(8,128)} custom-call(s32[8192]{0:T(1024)} %lab_ref.9, f32[8192,32]{1,0:T(8,128)} %subtract_exponential_fusion.w_ref), custom_call_target="tpu_custom_call" | custom-call | tf_op jit(solution)/shard_map/pallas_call | solution.py:85
  537.9 9.8 %collective-permute-done.50 = f32[32,1025]{1,0:T(8,128)S(1)} collective-permute-done((f32[32,1025]{1,0:T(8,128)S(1)}, f32[32,1025]{1,0:T(8,128)S(1)}, u32[]{:S(2)}, u32[]{:S(2)}) %collective-permute-start.50) | collective-permute-done | bytes 131232 | tf_op jit(solution)/shard_map/ppermute | solution.py:29
  (318 shorter events, 264.0 us)
Async XLA Ops:
  24.9 12.7 %collective-permute-start = (f32[32,1024]{0,1:T(8,128)S(1)}, f32[32,1024]{0,1:T(8,128)S(1)}, u32[]{:S(2)}, u32[]{:S(2)}) collective-permute-start(f32[32,1024]{0,1:T(8,128)S(1)} %get-tuple-element.53), channel_id=1, source_target_pairs={{0,1},{1,0},{2,3},{3,2},{4,5},{5,4},{6,7},{7,6},{8,9},{9,8},{10,11... | collective-permute-start | bytes 393224 | tf_op jit(solution)/shard_map/ppermute | solution.py:47
  27.0 25.2 %collective-permute-start.1 = (f32[32,1024]{0,1:T(8,128)S(1)}, f32[32,1024]{0,1:T(8,128)}, u32[]{:S(2)}, u32[]{:S(2)}) collective-permute-start(f32[32,1024]{0,1:T(8,128)S(1)} %get-tuple-element.55), channel_id=1, source_target_pairs={{0,2},{1,3},{2,0},{3,1},{4,6},{5,7},{6,4},{7,5},{8,10},{9,11},{10,... | collective-permute-start | bytes 393224 | tf_op jit(solution)/shard_map/ppermute | solution.py:47
  29.5 24.8 %collective-permute-start.2 = (f32[32,1024]{0,1:T(8,128)S(1)}, f32[32,1024]{0,1:T(8,128)}, u32[]{:S(2)}, u32[]{:S(2)}) collective-permute-start(f32[32,1024]{0,1:T(8,128)S(1)} %get-tuple-element.54), channel_id=1, source_target_pairs={{0,3},{1,2},{2,1},{3,0},{4,7},{5,6},{6,5},{7,4},{8,11},{9,10},{10,... | collective-permute-start | bytes 393224 | tf_op jit(solution)/shard_map/ppermute | solution.py:47
  95.0 25.9 %collective-permute-start.9 = (f32[32,2048]{1,0:T(8,128)S(1)}, f32[32,2048]{1,0:T(8,128)S(1)}, u32[]{:S(2)}, u32[]{:S(2)}) collective-permute-start(f32[32,2048]{1,0:T(8,128)S(1)} %copy.253), channel_id=1, source_target_pairs={{0,64},{4,68},{8,72},{12,76},{16,80},{20,84},{24,88},{28,92},{32,9... | collective-permute-start | bytes 786440 | tf_op jit(solution)/shard_map/ppermute | solution.py:29
  98.3 23.0 %collective-permute-start.10 = (f32[32,2048]{1,0:T(8,128)S(1)}, f32[32,2048]{1,0:T(8,128)S(1)}, u32[]{:S(2)}, u32[]{:S(2)}) collective-permute-start(f32[32,2048]{1,0:T(8,128)S(1)} %copy.253), channel_id=1, source_target_pairs={{0,128},{4,132},{8,136},{12,140},{16,144},{20,148},{24,152},{28,15... | collective-permute-start | bytes 786440 | tf_op jit(solution)/shard_map/ppermute | solution.py:29
  103.1 19.6 %collective-permute-start.11 = (f32[32,2048]{1,0:T(8,128)S(1)}, f32[32,2048]{1,0:T(8,128)S(1)}, u32[]{:S(2)}, u32[]{:S(2)}) collective-permute-start(f32[32,2048]{1,0:T(8,128)S(1)} %copy.253), channel_id=1, source_target_pairs={{0,192},{4,196},{8,200},{12,204},{16,208},{20,212},{24,216},{28,22... | collective-permute-start | bytes 786440 | tf_op jit(solution)/shard_map/ppermute | solution.py:29
  128.1 21.1 %collective-permute-start.13 = (f32[32,1024]{0,1:T(8,128)}, f32[32,1024]{0,1:T(8,128)}, u32[]{:S(2)}, u32[]{:S(2)}) collective-permute-start(f32[32,1024]{0,1:T(8,128)} %get-tuple-element.46), channel_id=1, source_target_pairs={{0,2},{1,3},{2,0},{3,1},{4,6},{5,7},{6,4},{7,5},{8,10},{9,11},{10,... | collective-permute-start | bytes 393224 | tf_op jit(solution)/shard_map/ppermute | solution.py:59
  133.1 23.9 %collective-permute-start.14 = (f32[32,1024]{0,1:T(8,128)}, f32[32,1024]{0,1:T(8,128)S(1)}, u32[]{:S(2)}, u32[]{:S(2)}) collective-permute-start(f32[32,1024]{0,1:T(8,128)} %get-tuple-element.46), channel_id=1, source_target_pairs={{0,3},{1,2},{2,1},{3,0},{4,7},{5,6},{6,5},{7,4},{8,11},{9,10},{10,... | collective-permute-start | bytes 393224 | tf_op jit(solution)/shard_map/ppermute | solution.py:59
  206.7 16.9 %collective-permute-start.15 = (f32[32,1025]{1,0:T(8,128)S(1)}, f32[32,1025]{1,0:T(8,128)S(1)}, u32[]{:S(2)}, u32[]{:S(2)}) collective-permute-start(f32[32,1025]{1,0:T(8,128)S(1)} %get-tuple-element.64), channel_id=1, source_target_pairs={{0,1},{1,0},{2,3},{3,2},{4,5},{5,4},{6,7},{7,6},{8,9},{9,8},{10,11... | collective-permute-start | bytes 393608 | tf_op jit(solution)/shard_map/ppermute | solution.py:47
  267.2 14.8 %collective-permute-start.24 = (f32[32,1025]{1,0:T(8,128)S(1)}, f32[32,1025]{1,0:T(8,128)S(1)}, u32[]{:S(2)}, u32[]{:S(2)}) collective-permute-start(f32[32,1025]{1,0:T(8,128)S(1)} %pad_maximum_fusion.9), channel_id=1, source_target_pairs={{0,64},{4,68},{8,72},{12,76},{16,80},{20,84},{24,88},{28,92},{32,9... | collective-permute-start | bytes 393608 | tf_op jit(solution)/shard_map/ppermute | solution.py:29
  268.9 13.3 %collective-permute-start.25 = (f32[32,1025]{1,0:T(8,128)S(1)}, f32[32,1025]{1,0:T(8,128)S(1)}, u32[]{:S(2)}, u32[]{:S(2)}) collective-permute-start(f32[32,1025]{1,0:T(8,128)S(1)} %pad_maximum_fusion.9), channel_id=1, source_target_pairs={{0,128},{4,132},{8,136},{12,140},{16,144},{20,148},{24,152},{28,15... | collective-permute-start | bytes 393608 | tf_op jit(solution)/shard_map/ppermute | solution.py:29
  272.4 12.9 %collective-permute-start.26 = (f32[32,1025]{1,0:T(8,128)S(1)}, f32[32,1025]{1,0:T(8,128)S(1)}, u32[]{:S(2)}, u32[]{:S(2)}) collective-permute-start(f32[32,1025]{1,0:T(8,128)S(1)} %pad_maximum_fusion.9), channel_id=1, source_target_pairs={{0,192},{4,196},{8,200},{12,204},{16,208},{20,212},{24,216},{28,22... | collective-permute-start | bytes 393608 | tf_op jit(solution)/shard_map/ppermute | solution.py:29
  302.5 13.4 %collective-permute-start.29 = (f32[32,1024]{0,1:T(8,128)S(1)}, f32[32,1024]{0,1:T(8,128)S(1)}, u32[]{:S(2)}, u32[]{:S(2)}) collective-permute-start(f32[32,1024]{0,1:T(8,128)S(1)} %copy.300), channel_id=1, source_target_pairs={{0,8},{4,12},{8,0},{12,4},{16,24},{20,28},{24,16},{28,20},{32,40},... | collective-permute-start | bytes 393224 | tf_op jit(solution)/shard_map/ppermute | solution.py:29
  304.2 23.4 %collective-permute-start.30 = (f32[32,1024]{0,1:T(8,128)S(1)}, f32[32,1024]{0,1:T(8,128)S(1)}, u32[]{:S(2)}, u32[]{:S(2)}) collective-permute-start(f32[32,1024]{0,1:T(8,128)S(1)} %copy.300), channel_id=1, source_target_pairs={{0,12},{4,8},{8,4},{12,0},{16,28},{20,24},{24,20},{28,16},{32,44},... | collective-permute-start | bytes 393224 | tf_op jit(solution)/shard_map/ppermute | solution.py:29
  327.7 17.8 %collective-permute-start.31 = (f32[32,1024]{0,1:T(8,128)S(1)}, f32[32,1024]{0,1:T(8,128)S(1)}, u32[]{:S(2)}, u32[]{:S(2)}) collective-permute-start(f32[32,1024]{0,1:T(8,128)S(1)} %add_add_fusion.4), channel_id=1, source_target_pairs={{0,16},{4,20},{8,24},{12,28},{16,0},{20,4},{24,8},{28,12},{32,48},... | collective-permute-start | bytes 393224 | tf_op jit(solution)/shard_map/ppermute | solution.py:29
  333.4 16.0 %collective-permute-start.32 = (f32[32,1024]{0,1:T(8,128)S(1)}, f32[32,1024]{0,1:T(8,128)S(1)}, u32[]{:S(2)}, u32[]{:S(2)}) collective-permute-start(f32[32,1024]{0,1:T(8,128)S(1)} %add_add_fusion.4), channel_id=1, source_target_pairs={{0,32},{4,36},{8,40},{12,44},{16,48},{20,52},{24,56},{28,60},{32,0... | collective-permute-start | bytes 393224 | tf_op jit(solution)/shard_map/ppermute | solution.py:29
  337.5 23.2 %collective-permute-start.33 = (f32[32,1024]{0,1:T(8,128)S(1)}, f32[32,1024]{0,1:T(8,128)S(1)}, u32[]{:S(2)}, u32[]{:S(2)}) collective-permute-start(f32[32,1024]{0,1:T(8,128)S(1)} %add_add_fusion.4), channel_id=1, source_target_pairs={{0,48},{4,52},{8,56},{12,60},{16,32},{20,36},{24,40},{28,44},{32,1... | collective-permute-start | bytes 393224 | tf_op jit(solution)/shard_map/ppermute | solution.py:29
  360.8 47.7 %collective-permute-start.34 = (f32[32,1024]{0,1:T(8,128)S(1)}, f32[32,1024]{0,1:T(8,128)S(1)}, u32[]{:S(2)}, u32[]{:S(2)}) collective-permute-start(f32[32,1024]{0,1:T(8,128)S(1)} %add_add_fusion.3), channel_id=1, source_target_pairs={{0,64},{4,68},{8,72},{12,76},{16,80},{20,84},{24,88},{28,92},{32,9... | collective-permute-start | bytes 393224 | tf_op jit(solution)/shard_map/ppermute | solution.py:29
  362.4 51.5 %collective-permute-start.35 = (f32[32,1024]{0,1:T(8,128)S(1)}, f32[32,1024]{0,1:T(8,128)S(1)}, u32[]{:S(2)}, u32[]{:S(2)}) collective-permute-start(f32[32,1024]{0,1:T(8,128)S(1)} %add_add_fusion.3), channel_id=1, source_target_pairs={{0,128},{4,132},{8,136},{12,140},{16,144},{20,148},{24,152},{28,15... | collective-permute-start | bytes 393224 | tf_op jit(solution)/shard_map/ppermute | solution.py:29
  369.0 45.3 %collective-permute-start.36 = (f32[32,1024]{0,1:T(8,128)S(1)}, f32[32,1024]{0,1:T(8,128)S(1)}, u32[]{:S(2)}, u32[]{:S(2)}) collective-permute-start(f32[32,1024]{0,1:T(8,128)S(1)} %add_add_fusion.3), channel_id=1, source_target_pairs={{0,192},{4,196},{8,200},{12,204},{16,208},{20,212},{24,216},{28,22... | collective-permute-start | bytes 393224 | tf_op jit(solution)/shard_map/ppermute | solution.py:29
  415.4 21.4 %collective-permute-start.38 = (f32[32,1024]{0,1:T(8,128)S(1)}, f32[32,1024]{0,1:T(8,128)S(1)}, u32[]{:S(2)}, u32[]{:S(2)}) collective-permute-start(f32[32,1024]{0,1:T(8,128)S(1)} %get-tuple-element.29), channel_id=1, source_target_pairs={{0,2},{1,3},{2,0},{3,1},{4,6},{5,7},{6,4},{7,5},{8,10},{9,11},{10,... | collective-permute-start | bytes 393224 | tf_op jit(solution)/shard_map/ppermute | solution.py:59
  415.4 25.6 %collective-permute-start.39 = (f32[32,1024]{0,1:T(8,128)S(1)}, f32[32,1024]{0,1:T(8,128)S(1)}, u32[]{:S(2)}, u32[]{:S(2)}) collective-permute-start(f32[32,1024]{0,1:T(8,128)S(1)} %get-tuple-element.29), channel_id=1, source_target_pairs={{0,3},{1,2},{2,1},{3,0},{4,7},{5,6},{6,5},{7,4},{8,11},{9,10},{10,... | collective-permute-start | bytes 393224 | tf_op jit(solution)/shard_map/ppermute | solution.py:59
  530.9 16.8 %collective-permute-start.50 = (f32[32,1025]{1,0:T(8,128)S(1)}, f32[32,1025]{1,0:T(8,128)S(1)}, u32[]{:S(2)}, u32[]{:S(2)}) collective-permute-start(f32[32,1025]{1,0:T(8,128)S(1)} %pad_maximum_fusion.12), channel_id=1, source_target_pairs={{0,128},{4,132},{8,136},{12,140},{16,144},{20,148},{24,152},{28,15... | collective-permute-start | bytes 393608 | tf_op jit(solution)/shard_map/ppermute | solution.py:29
  536.4 13.0 %collective-permute-start.51 = (f32[32,1025]{1,0:T(8,128)S(1)}, f32[32,1025]{1,0:T(8,128)S(1)}, u32[]{:S(2)}, u32[]{:S(2)}) collective-permute-start(f32[32,1025]{1,0:T(8,128)S(1)} %pad_maximum_fusion.12), channel_id=1, source_target_pairs={{0,192},{4,196},{8,200},{12,204},{16,208},{20,212},{24,216},{28,22... | collective-permute-start | bytes 393608 | tf_op jit(solution)/shard_map/ppermute | solution.py:29
  (38 other events, 402.0 us)
